TPU v7x, 256 devices: a whole 4x4x8 slice. The times are simulated.
256 devices in a mesh: rows: 64 (over y, z, core), rhs: 4 (over x).
Axes of the slice: x: 4, y: 4, z: 8, core: 2. Of those that a mesh axis runs over, the one named last changes fastest.
Arguments:
- kernel_rows: bfloat16 [131072, 512], P(('rows', 'rhs')), may hold values from 0 to 1
- factor_blocks: bfloat16 [512, 8, 256, 256], P('rows'), may hold values from -0.125 to 0.125
- diag_inverse: bfloat16 [512, 256, 256], P('rows'), as said below
- pattern: int32 [512, 8], P('rows'), may hold values from 0 to 511, as said below
- live_counts: int32 [512], P('rows'), may hold values from 0 to 8, as said below
Outputs:
- solution: bfloat16 [131072, 512], P('rows', 'rhs')
Inputs may be any that keep to these rules, and one draw needn't show every extreme that they name: pattern[s, k] names a block row of a lower level than s; slot 0 of every block row above level 0 names a block row of the level just below; rows of level 0 hold 0. Block row t is held by index t // 8 of rows; the used slots of the block rows held by one index of rows name, for any one level, at most 1 distinct block rows held by any one other index. `live_counts`: 0 on level 0, from 1 to 8 on higher levels, 8 reached. `diag_inverse`: each block is the inverse of a well-conditioned diagonal block of the factor.
All inputs are finite; a program needn't handle non-finite values.
Results may differ from a plain program's by a relative error of at most 0.0058.
Values may be sent and summed in bfloat16 or wider, within the bound.
No kernel may reach another device: no remote copies, remote signals or barrier semaphores. Data moves between devices by JAX's collectives and lax.ppermute only.
A program may use at most 128 MiB of HBM per device.

v0:
```python
import jax
import jax.numpy as jnp
from jax import lax
from jax.sharding import PartitionSpec as P

LEV = 4


def shards(kernel_rows, factor_blocks, diag_inverse, pattern, live_counts):
    received = lax.all_to_all(kernel_rows, "rhs", split_axis=1, concat_axis=0, tiled=True)
    per_device = factor_blocks.shape[0]
    slot_count = factor_blocks.shape[1]
    block = factor_blocks.shape[2]
    width = received.shape[1]
    right_side = received.reshape(per_device, block, width)
    holders = lax.axis_size("rows")
    per_level = per_device // LEV
    level_size = holders * per_level
    level_of = pattern % per_device // per_level
    holder_of = pattern // per_device
    offset_of = pattern % per_level
    active = jnp.arange(slot_count)[None, :] < live_counts[:, None]
    position = holder_of * per_level + offset_of
    flat_index = level_of * level_size + position
    gathered_all = []
    solved_all = []
    for level_now in range(LEV):
        lower = level_now * per_level
        upper = lower + per_level
        if level_now == 0:
            summed_now = jnp.zeros((per_level, block, width), jnp.float32)
        else:
            available = jnp.concatenate(gathered_all, axis=0)
            picked = jnp.take(available, flat_index[lower:upper], axis=0, mode="clip")
            picked = jnp.where(active[lower:upper, :, None, None], picked, jnp.zeros_like(picked))
            summed_now = jnp.einsum(
                "bkij,bkjr->bir",
                factor_blocks[lower:upper],
                picked,
                preferred_element_type=jnp.float32,
            )
        residual = (right_side[lower:upper].astype(jnp.float32) - summed_now).astype(jnp.bfloat16)
        solved = jnp.einsum(
            "bij,bjr->bir", diag_inverse[lower:upper], residual, preferred_element_type=jnp.float32
        ).astype(jnp.bfloat16)
        solved_all.append(solved)
        if level_now + 1 < LEV:
            incoming = lax.all_gather(solved, "rows", axis=0, tiled=True)
            gathered_all.append(incoming)
    return jnp.concatenate(solved_all, axis=0).reshape(per_device * block, width)


def solution(mesh):
    placed = (
        P(("rows", "rhs"), None),
        P("rows", None, None, None),
        P("rows", None, None),
        P("rows", None),
        P("rows"),
    )
    return jax.shard_map(
        shards, mesh=mesh, in_specs=placed, out_specs=P("rows", "rhs"), check_vma=False
    )
```

profile of v0, /device:TPU:2, one launch (start us, length us, event | category | flops | bytes accessed | tf_op | source)
XLA Modules:
  0.0 338.1 jit_solution(18205425547887080133)
XLA Ops:
  6.5 1.3 copy.30
  7.8 12.6 %all_to_all.16 = bf16[512,4,128]{0,2,1:T(8,128)(2,1)S(1)} all-to-all(bf16[512,4,128]{0,2,1:T(8,128)(2,1)S(1)} %bitcast.60), channel_id=1, replica_groups=mesh['rows'=64,'rhs'=4] {'rhs'}, dimensions={1} | all-to-all | bytes 1048576 | tf_op jit(solution)/shard_map/all_to_all | solution.py:10
  20.4 0.1 fusion.84
  20.5 0.1 copy.31
  20.6 1.8 convolution_convert_fusion
  22.5 0.0 all-gather.6.cloned.1.call-start
  22.5 0.7 fusion.71
  23.3 0.1 reshape.28
  23.3 0.7 iota_compare_fusion
  24.1 0.1 copy.32
  24.2 0.1 copy.34
  24.4 83.4 %all-gather.4.cloned.1.call-done = bf16[128,256,128]{2,1,0:T(8,128)(2,1)} async-done(((bf16[2,256,128]{2,1,0:T(8,128)(2,1)}), bf16[128,256,128]{2,1,0:T(8,128)(2,1)}) %all-gather.4.cloned.1.call-update) | async-done | bytes 8388624 | tf_op jit(solution)/shard_map/all_gather | solution.py:48
  107.7 4.1 %gather_fusion = bf16[16,256,128]{2,1,0:T(8,128)(2,1)S(1)} fusion(bf16[128,256,128]{2,1,0:T(8,128)(2,1)} %all-gather.4.cloned.1.call-done, s32[1024]{0:T(1024)S(1)} %pad_clamp_fusion.2), kind=kCustom, calls=%fused_computation | custom fusion | bytes 2097216 | tf_op jit(solution)/shard_map/jit(_take)/gather | solution.py:34
  111.8 0.5 copy.33
  112.4 3.3 fusion.39
  115.7 0.1 reshape.36
  115.8 0.1 copy.36
  115.9 0.8 copy.38
  116.8 79.4 %all-gather.6.cloned.1.call-done = bf16[128,256,128]{2,1,0:T(8,128)(2,1)} async-done(((bf16[2,256,128]{2,1,0:T(8,128)(2,1)}), bf16[128,256,128]{2,1,0:T(8,128)(2,1)}) %all-gather.6.cloned.1.call-update) | async-done | bytes 8388624 | tf_op jit(solution)/shard_map/all_gather | solution.py:48
  196.1 13.9 %pad_maximum_fusion.1 = bf16[256,256,128]{2,1,0:T(8,128)(2,1)} fusion(bf16[128,256,128]{2,1,0:T(8,128)(2,1)} %all-gather.6.cloned.1.call-done, bf16[128,256,128]{2,1,0:T(8,128)(2,1)} %all-gather.4.cloned.1.call-done), kind=kLoop, calls=%fused_computation.4 | loop fusion | flops 8388608 | bytes 33554432 | tf_op jit(solution)/shard_map/concatenate | solution.py:33
  210.0 6.5 %gather_fusion.1 = bf16[16,256,128]{2,1,0:T(8,128)(2,1)S(1)} fusion(bf16[256,256,128]{2,1,0:T(8,128)(2,1)} %pad_maximum_fusion.1, s32[1024]{0:T(1024)S(1)} %pad_clamp_fusion.1), kind=kCustom, calls=%fused_computation.1 | custom fusion | bytes 2097216 | tf_op jit(solution)/shard_map/jit(_take)/gather | solution.py:34
  216.6 0.5 copy.37
  217.1 3.3 fusion.42
  220.4 0.1 reshape.44
  220.5 0.1 copy.40
  220.6 0.8 copy.42
  221.5 79.4 %all-gather.8.cloned.1.call-done = bf16[128,256,128]{2,1,0:T(8,128)(2,1)} async-done(((bf16[2,256,128]{2,1,0:T(8,128)(2,1)}), bf16[128,256,128]{2,1,0:T(8,128)(2,1)}) %all-gather.8.cloned.1.call-update) | async-done | bytes 8388624 | tf_op jit(solution)/shard_map/all_gather | solution.py:48
  300.9 17.7 %pad_maximum_fusion = bf16[384,256,128]{2,1,0:T(8,128)(2,1)} fusion(bf16[128,256,128]{2,1,0:T(8,128)(2,1)} %all-gather.8.cloned.1.call-done, bf16[128,256,128]{2,1,0:T(8,128)(2,1)} %all-gather.6.cloned.1.call-done, bf16[128,256,128]{2,1,0:T(8,128)(2,1)} %all-gather.4.cloned.1.call-done), kind=kLoop, calls=%fused_computation.3 | loop fusion | flops 25165824 | bytes 50331648 | tf_op jit(solution)/shard_map/concatenate | solution.py:33
  318.6 9.0 %gather_fusion.2 = bf16[16,256,128]{2,1,0:T(8,128)(2,1)S(1)} fusion(bf16[384,256,128]{2,1,0:T(8,128)(2,1)} %pad_maximum_fusion, s32[1024]{0:T(1024)S(1)} %pad_clamp_fusion), kind=kCustom, calls=%fused_computation.2 | custom fusion | bytes 2097216 | tf_op jit(solution)/shard_map/jit(_take)/gather | solution.py:34
  327.6 0.5 copy.41
  328.1 2.6 fusion.45
  330.8 0.9 pad_maximum_fusion.2
  (18 shorter events, 0.2 us)
Async XLA Ops:
  6.5 101.2 %all-gather.4.cloned.1.call-start = ((), (), s32[]{:S(2)}) async-start(), calls=%async_computation.1 | async-start | bytes 8519680 | tf_op jit(solution)/shard_map/all_gather | solution.py:48
  22.5 173.7 %all-gather.6.cloned.1.call-start = ((), (), s32[]{:S(2)}) async-start(), calls=%async_computation.2 | async-start | bytes 8519680 | tf_op jit(solution)/shard_map/all_gather | solution.py:48
  115.7 185.2 %all-gather.8.cloned.1.call-start = ((), (), s32[]{:S(2)}) async-start(), calls=%async_computation.3 | async-start | bytes 8519680 | tf_op jit(solution)/shard_map/all_gather | solution.py:48
  116.8 100.3 %copy-start.3 = (bf16[8,256,256]{2,1,0:T(8,128)(2,1)S(1)}, bf16[8,256,256]{2,1,0:T(8,128)(2,1)}, u32[]{:S(2)}) copy-start(bf16[8,256,256]{2,1,0:T(8,128)(2,1)} %param.7) | copy-start | bytes 3145732
  318.6 12.2 %copy-start = (bf16[2,256,128]{2,1,0:T(8,128)(2,1)S(1)}, bf16[2,256,128]{2,1,0:T(8,128)(2,1)}, u32[]{:S(2)}) copy-start(bf16[2,256,128]{2,1,0:T(8,128)(2,1)} %convolution_convert_fusion) | copy-start | bytes 393220
  318.6 12.2 %copy-start.1 = (bf16[2,256,128]{2,1,0:T(8,128)(2,1)S(1)}, bf16[2,256,128]{2,1,0:T(8,128)(2,1)}, u32[]{:S(2)}) copy-start(bf16[2,256,128]{2,1,0:T(8,128)(2,1)} %fusion.39) | copy-start | bytes 393220
  318.6 12.2 %copy-start.2 = (bf16[2,256,128]{2,1,0:T(8,128)(2,1)S(1)}, bf16[2,256,128]{2,1,0:T(8,128)(2,1)}, u32[]{:S(2)}) copy-start(bf16[2,256,128]{2,1,0:T(8,128)(2,1)} %fusion.42) | copy-start | bytes 393220
Sparse Core Ops, SparseCore 0:
  22.6 85.0 all-gather.3
  115.8 80.2 all-gather.5
  220.5 80.2 all-gather.7
where the time goes:
time: 340 us; the launch traced here: 338 us
  waiting for transfers between devices  242 us (71%)
  other arithmetic  34 us (10%)
  local copies, waits for them, and re-layouts  25 us (7%)
  between operations  13.3 us (4%)
  blocking collectives  12.6 us (4%)
  matrix products  11 us (3%)
    all_gather x3, waiting for transfers between devices, shards(): incoming = lax.all_gather(solved, 'rows', axis=0, tiled=True)  242 us
    concatenate x2, other arithmetic, shards(): available = jnp.concatenate(gathered_all, axis=0)  31.6 us
    gather x6, local copies, waits for them, and re-layouts, shards(): picked = jnp.take(available, flat_index[lower:upper], axis=0, mode='clip')  21.2 us
    all_to_all x1, blocking collectives, shards(): lax.all_to_all(kernel_rows, 'rhs', split_axis=1, concat_axis=0, tiled=True)  12.6 us
    dot_general x4, matrix products, shards(): jnp.einsum('bij,bjr->bir', diag_inverse[lower:upper], residual, preferred...  11 us
  transfers between devices with their start and end apart: 3, of which 3 were waited for; matrix products, arithmetic and copies ran while one was open for 1% of the time, Pallas kernels for 0%

commit v1 on v0

v1 whole, which is shorter than its diff:
```python
import jax
import jax.numpy as jnp
import numpy as np
from jax import lax
from jax.sharding import Mesh
from jax.sharding import PartitionSpec as P

LEV = 4
ROWS = ("y", "z", "core")


def ring(n, step):
    return [(i, (i + step) % n) for i in range(n)]


def ring_gather(x, axis, n):
    got = [None] * n
    got[0] = x
    fwd = x
    bwd = x
    for k in range(1, (n - 1) // 2 + 1):
        fwd = lax.ppermute(fwd, axis, ring(n, 1))
        got[n - k] = fwd
        bwd = lax.ppermute(bwd, axis, ring(n, -1))
        got[k] = bwd
    if n % 2 == 0 and n > 1:
        m = fwd.shape[0] // 2
        far_f = lax.ppermute(fwd[:m], axis, ring(n, 1))
        far_b = lax.ppermute(bwd[m:], axis, ring(n, -1))
        got[n // 2] = jnp.concatenate([far_f, far_b], 0)
    return jnp.stack(got)


def gather_level(solved, ny, nz):
    core = lax.axis_index("core")
    other = lax.ppermute(solved, "core", ring(2, 1))
    chip = jnp.where(core == 0, jnp.stack([solved, other]), jnp.stack([other, solved]))
    half = chip.shape[-1] // 2
    part_a = ring_gather(ring_gather(chip[..., :half], "z", nz), "y", ny)
    part_b = ring_gather(ring_gather(chip[..., half:], "y", ny), "z", nz)
    return part_a.reshape(-1, *part_a.shape[-2:]), part_b.reshape(-1, *part_b.shape[-2:])


def make_shards(ny, nz):
    def shards(kernel_rows, factor_blocks, diag_inverse, pattern, live_counts):
        received = lax.all_to_all(kernel_rows, "x", split_axis=1, concat_axis=0, tiled=True)
        per_device = factor_blocks.shape[0]
        slot_count = factor_blocks.shape[1]
        block = factor_blocks.shape[2]
        width = received.shape[1]
        right_side = received.reshape(per_device, block, width)
        per_level = per_device // LEV
        level_of = pattern % per_device // per_level
        holder_of = pattern // per_device
        offset_of = pattern % per_level
        active = jnp.arange(slot_count)[None, :] < live_counts[:, None]
        my_y = lax.axis_index("y")
        my_z = lax.axis_index("z")
        hy = holder_of // (nz * 2)
        hz = holder_of // 2 % nz
        hc = holder_of % 2
        jy = (hy - my_y) % ny
        jz = (hz - my_z) % nz
        index_a = ((jy * nz + jz) * 2 + hc) * per_level + offset_of
        index_b = ((jz * ny + jy) * 2 + hc) * per_level + offset_of
        gathered = []
        solved_all = []
        for level_now in range(LEV):
            lower = level_now * per_level
            upper = lower + per_level
            if level_now == 0:
                summed_now = jnp.zeros((per_level, block, width), jnp.float32)
            else:
                ia = index_a[lower:upper]
                ib = index_b[lower:upper]
                lv = level_of[lower:upper]
                picked = None
                for source, (part_a, part_b) in enumerate(gathered):
                    take_a = jnp.take(part_a, ia, axis=0, mode="clip")
                    take_b = jnp.take(part_b, ib, axis=0, mode="clip")
                    both = jnp.concatenate([take_a, take_b], -1)
                    keep = (lv == source)[:, :, None, None]
                    both = jnp.where(keep, both, jnp.zeros_like(both))
                    picked = both if picked is None else picked + both
                picked = jnp.where(active[lower:upper, :, None, None], picked, jnp.zeros_like(picked))
                summed_now = jnp.einsum(
                    "bkij,bkjr->bir",
                    factor_blocks[lower:upper],
                    picked,
                    preferred_element_type=jnp.float32,
                )
            residual = (right_side[lower:upper].astype(jnp.float32) - summed_now).astype(jnp.bfloat16)
            solved = jnp.einsum(
                "bij,bjr->bir", diag_inverse[lower:upper], residual, preferred_element_type=jnp.float32
            ).astype(jnp.bfloat16)
            solved_all.append(solved)
            if level_now + 1 < LEV:
                gathered.append(gather_level(solved, ny, nz))
        return jnp.concatenate(solved_all, axis=0).reshape(per_device * block, width)

    return shards


def solution(mesh):
    rows = mesh.shape["rows"]
    devices = mesh.devices
    try:
        ny = len({d.coords[1] for d in devices.flat})
        nz = len({d.coords[2] for d in devices.flat})
    except Exception:
        ny, nz = 4, rows // 8
    fine = Mesh(devices.reshape(ny, nz, rows // (ny * nz), mesh.shape["rhs"]), ROWS + ("x",))
    placed = (
        P(ROWS + ("x",), None),
        P(ROWS, None, None, None),
        P(ROWS, None, None),
        P(ROWS, None),
        P(ROWS),
    )
    return jax.shard_map(
        make_shards(ny, nz), mesh=fine, in_specs=placed, out_specs=P(ROWS, "x"), check_vma=False
    )
```

time: 340 us -> 342 us (level); the launches traced: 338 us -> 336 us
  waiting for transfers between devices: 242 us -> 88.5 us
  starting transfers between devices: 0.09 us -> 117 us
  local copies, waits for them, and re-layouts: 25 us -> 94.5 us
  blocking collectives: 12.6 us -> 0 us
  between operations: 13.3 us -> 1.21 us
  other arithmetic: 34 us -> 25.7 us
    all_gather x3 -> x0, waiting for transfers between devices: 242 us -> none  [shards(): incoming = lax.all_gather(solved, 'rows', axis=0, tiled=True)]
    ppermute x0 -> x75, starting transfers between devices: none -> 111 us  [the longest x24 59.7 us: ring_gather(): bwd = lax.ppermute(bwd, axis, ring(n, -1))]
    ppermute x0 -> x75, waiting for transfers between devices: none -> 83.4 us  [the longest x24 50.2 us: ring_gather(): bwd = lax.ppermute(bwd, axis, ring(n, -1))]
    unnamed x9 -> x100, local copies, waits for them, and re-layouts: 1.27 us -> 35.2 us
    concatenate x2 -> x0, other arithmetic: 31.6 us -> none  [shards(): available = jnp.concatenate(gathered_all, axis=0)]
    gather x6 -> x12, local copies, waits for them, and re-layouts: 21.2 us -> 35.6 us  [the longest x6 18.2 us: shards(): take_b = jnp.take(part_b, ib, axis=0, mode='clip')]
    another operation x0 -> x12, other arithmetic: none -> 13 us  [ring_gather(): return jnp.stack(got)]
    all_to_all x1 -> x0, blocking collectives: 12.6 us -> none  [shards(): lax.all_to_all(kernel_rows, 'rhs', split_axis=1, concat_axis=0, tiled=True)]
  transfers between devices with their start and end apart: 3 -> 76, of which waited for: 3 -> 25; matrix products, arithmetic and copies ran while one was open for 1% -> 27% of each run, Pallas kernels for 0% -> 0%
where the time goes in v1:
time: 342 us; the launch traced here: 336 us
  starting transfers between devices  117 us (34%)
  local copies, waits for them, and re-layouts  94.5 us (28%)
  waiting for transfers between devices  88.5 us (26%)
  other arithmetic  25.7 us (8%)
  matrix products  9.34 us (3%)
    ppermute x24, starting transfers between devices, ring_gather(): bwd = lax.ppermute(bwd, axis, ring(n, -1))  59.7 us
    ppermute x24, waiting for transfers between devices, ring_gather(): bwd = lax.ppermute(bwd, axis, ring(n, -1))  50.2 us
    unnamed x100, local copies, waits for them, and re-layouts  35.2 us
    ppermute x12, starting transfers between devices, ring_gather(): far_b = lax.ppermute(bwd[m:], axis, ring(n, -1))  30.1 us
    ppermute x12, waiting for transfers between devices, ring_gather(): far_f = lax.ppermute(fwd[:m], axis, ring(n, 1))  19.7 us
    gather x6, local copies, waits for them, and re-layouts, shards(): take_b = jnp.take(part_b, ib, axis=0, mode='clip')  18.2 us
    gather x6, local copies, waits for them, and re-layouts, shards(): take_a = jnp.take(part_a, ia, axis=0, mode='clip')  17.5 us
    ppermute x24, starting transfers between devices, ring_gather(): fwd = lax.ppermute(fwd, axis, ring(n, 1))  15.6 us
  transfers between devices with their start and end apart: 76, of which 25 were waited for; matrix products, arithmetic and copies ran while one was open for 27% of the time, Pallas kernels for 0%

profile of v1, /device:TPU:2, one launch (start us, length us, event | category | flops | bytes accessed | tf_op | source)
XLA Modules:
  0.0 335.8 jit_solution(9833101026547209130)
XLA Ops:
  2.1 5.7 %all-to-all-start = ((bf16[512,4,128]{0,2,1:T(8,128)(2,1)}), bf16[512,4,128]{0,2,1:T(8,128)(2,1)S(1)}, u32[]{:S(2)}, u32[]{:S(2)}) async-start(bf16[512,4,128]{0,2,1:T(8,128)(2,1)} %bitcast), calls=%async_computation | async-start | bytes 1048576 | tf_op jit(solution)/shard_map/all_to_all | solution.py:46
  9.7 5.2 %all-to-all-done = bf16[512,4,128]{0,2,1:T(8,128)(2,1)S(1)} async-done(((bf16[512,4,128]{0,2,1:T(8,128)(2,1)}), bf16[512,4,128]{0,2,1:T(8,128)(2,1)S(1)}, u32[]{:S(2)}, u32[]{:S(2)}) %all-to-all-start) | async-done | bytes 524320 | tf_op jit(solution)/shard_map/all_to_all | solution.py:46
  18.6 5.9 %collective-permute-start.1 = (bf16[2,2,256,64]{2,3,1,0:T(8,128)(2,1)S(1)}, bf16[2,2,256,64]{2,3,1,0:T(8,128)(2,1)S(1)}, u32[]{:S(2)}, u32[]{:S(2)}) collective-permute-start(bf16[2,2,256,64]{2,3,1,0:T(8,128)(2,1)S(1)} %get-tuple-element.15), channel_id=1, source_target_pairs={{0,56},{8,0},{16,8},{24,16},{32,24},{40,32},{48,40},{56,48},{1,57}... | collective-permute-start | bytes 393224 | tf_op jit(solution)/shard_map/ppermute | solution.py:24
  30.4 3.8 %collective-permute-start.16 = (bf16[1,2,256,64]{2,3,1,0:T(8,128)(2,1)S(1)}, bf16[1,2,256,64]{2,3,1,0:T(8,128)(2,1)S(1)}, u32[]{:S(2)}, u32[]{:S(2)}) collective-permute-start(bf16[1,2,256,64]{2,3,1,0:T(8,128)(2,1)S(1)} %slice.252), channel_id=1, source_target_pairs={{0,192},{64,0},{128,64},{192,128},{1,193},{65,1},{129,65},{193,129... | collective-permute-start | bytes 196616 | tf_op jit(solution)/shard_map/ppermute | solution.py:29
  39.8 3.0 collective-permute-start.17
  42.9 3.2 collective-permute-start.3
  46.1 8.7 %collective-permute-done.3 = bf16[2,2,256,64]{2,3,1,0:T(8,128)(2,1)S(1)} collective-permute-done((bf16[2,2,256,64]{2,3,1,0:T(8,128)(2,1)S(1)}, bf16[2,2,256,64]{2,3,1,0:T(8,128)(2,1)S(1)}, u32[]{:S(2)}, u32[]{:S(2)}) %collective-permute-start.3) | collective-permute-done | bytes 131104 | tf_op jit(solution)/shard_map/ppermute | solution.py:24
  60.2 4.0 %collective-permute-done.7 = bf16[1,2,256,64]{2,3,1,0:T(8,128)(2,1)S(1)} collective-permute-done((bf16[1,2,256,64]{2,3,1,0:T(8,128)(2,1)S(1)}, bf16[1,2,256,64]{2,3,1,0:T(8,128)(2,1)S(1)}, u32[]{:S(2)}, u32[]{:S(2)}) %collective-permute-start.7) | collective-permute-done | bytes 65568 | tf_op jit(solution)/shard_map/ppermute | solution.py:28
  66.5 3.2 collective-permute-start.9
  70.4 7.6 %collective-permute-done.18 = bf16[4,2,2,256,64]{3,4,2,1,0:T(8,128)(2,1)} collective-permute-done((bf16[4,2,2,256,64]{3,4,2,1,0:T(8,128)(2,1)S(1)}, bf16[4,2,2,256,64]{3,4,2,1,0:T(8,128)(2,1)}, u32[]{:S(2)}, u32[]{:S(2)}) %collective-permute-start.18) | collective-permute-done | bytes 524320 | tf_op jit(solution)/shard_map/ppermute | solution.py:24
  97.9 3.2 collective-permute-start.12
  112.7 3.4 %pad_maximum_fusion = bf16[4,8,2,2,256,64]{4,5,3,2,1,0:T(8,128)(2,1)} fusion(bf16[1,8,2,2,256,64]{4,5,3,2,1,0:T(8,128)(2,1)S(1)} %bitcast.221, bf16[1,8,2,2,256,64]{4,5,3,2,1,0:T(8,128)(2,1)S(1)} %maximum_bitcast_fusion, bf16[1,8,2,2,256,64]{4,5,3,2,1,0:T(8,128)(2,1)S(1)} %bitcast.223, bf16[1,8,2,2,256,64]{4,5,3,2,1,0:T(8,128)(2,1)} %bitcast.242), kind=kLoop, calls=%fused_computation.12 | loop fusion | flops 6291456 | bytes 8388608 | tf_op jit(solution)/shard_map/stack | solution.py:31
  125.4 9.1 %collective-permute-start.38 = (bf16[2,2,256,64]{2,3,1,0:T(8,128)(2,1)S(1)}, bf16[2,2,256,64]{2,3,1,0:T(8,128)(2,1)S(1)}, u32[]{:S(2)}, u32[]{:S(2)}) collective-permute-start(bf16[2,2,256,64]{2,3,1,0:T(8,128)(2,1)S(1)} %get-tuple-element.14), channel_id=1, source_target_pairs={{0,192},{64,0},{128,64},{192,128},{1,193},{65,1},{129,65},{193,129... | collective-permute-start | bytes 393224 | tf_op jit(solution)/shard_map/ppermute | solution.py:24
  149.8 3.2 collective-permute-start.28
  153.7 7.9 %collective-permute-done.28 = bf16[2,2,256,64]{2,3,1,0:T(8,128)(2,1)S(1)} collective-permute-done((bf16[2,2,256,64]{2,3,1,0:T(8,128)(2,1)S(1)}, bf16[2,2,256,64]{2,3,1,0:T(8,128)(2,1)S(1)}, u32[]{:S(2)}, u32[]{:S(2)}) %collective-permute-start.28) | collective-permute-done | bytes 131104 | tf_op jit(solution)/shard_map/ppermute | solution.py:24
  166.6 3.7 %collective-permute-done.32 = bf16[1,2,256,64]{2,3,1,0:T(8,128)(2,1)S(1)} collective-permute-done((bf16[1,2,256,64]{2,3,1,0:T(8,128)(2,1)S(1)}, bf16[1,2,256,64]{2,3,1,0:T(8,128)(2,1)S(1)}, u32[]{:S(2)}, u32[]{:S(2)}) %collective-permute-start.32) | collective-permute-done | bytes 65568 | tf_op jit(solution)/shard_map/ppermute | solution.py:28
  172.9 3.1 collective-permute-start.34
  191.2 5.0 %collective-permute-done.35 = bf16[8,2,2,256,64]{3,4,2,1,0:T(8,128)(2,1)S(1)} collective-permute-done((bf16[8,2,2,256,64]{3,4,2,1,0:T(8,128)(2,1)}, bf16[8,2,2,256,64]{3,4,2,1,0:T(8,128)(2,1)S(1)}, u32[]{:S(2)}, u32[]{:S(2)}) %collective-permute-start.35) | collective-permute-done | bytes 1048608 | tf_op jit(solution)/shard_map/ppermute | solution.py:22
  196.5 3.3 collective-permute-start.37
  207.1 3.3 pad_maximum_fusion.1
  229.8 3.2 collective-permute-start.63
  235.6 3.8 %collective-permute-start.66 = (bf16[1,2,256,64]{2,3,1,0:T(8,128)(2,1)S(1)}, bf16[1,2,256,64]{2,3,1,0:T(8,128)(2,1)S(1)}, u32[]{:S(2)}, u32[]{:S(2)}) collective-permute-start(bf16[1,2,256,64]{2,3,1,0:T(8,128)(2,1)S(1)} %slice.274), channel_id=1, source_target_pairs={{0,192},{64,0},{128,64},{192,128},{1,193},{65,1},{129,65},{193,129... | collective-permute-start | bytes 196616 | tf_op jit(solution)/shard_map/ppermute | solution.py:29
  250.5 9.1 %collective-permute-done.53 = bf16[2,2,256,64]{2,3,1,0:T(8,128)(2,1)S(1)} collective-permute-done((bf16[2,2,256,64]{2,3,1,0:T(8,128)(2,1)S(1)}, bf16[2,2,256,64]{2,3,1,0:T(8,128)(2,1)S(1)}, u32[]{:S(2)}, u32[]{:S(2)}) %collective-permute-start.53) | collective-permute-done | bytes 131104 | tf_op jit(solution)/shard_map/ppermute | solution.py:24
  264.0 3.7 %collective-permute-done.57 = bf16[1,2,256,64]{2,3,1,0:T(8,128)(2,1)S(1)} collective-permute-done((bf16[1,2,256,64]{2,3,1,0:T(8,128)(2,1)S(1)}, bf16[1,2,256,64]{2,3,1,0:T(8,128)(2,1)S(1)}, u32[]{:S(2)}, u32[]{:S(2)}) %collective-permute-start.57) | collective-permute-done | bytes 65568 | tf_op jit(solution)/shard_map/ppermute | solution.py:28
  272.3 3.2 collective-permute-start.59
  275.6 5.7 %collective-permute-done.68 = bf16[4,2,2,256,64]{3,4,2,1,0:T(8,128)(2,1)} collective-permute-done((bf16[4,2,2,256,64]{3,4,2,1,0:T(8,128)(2,1)}, bf16[4,2,2,256,64]{3,4,2,1,0:T(8,128)(2,1)}, u32[]{:S(2)}, u32[]{:S(2)}) %collective-permute-start.68) | collective-permute-done | bytes 524320 | tf_op jit(solution)/shard_map/ppermute | solution.py:24
  290.0 3.6 %gather_fusion.8 = bf16[16,256,64]{1,2,0:T(8,128)(2,1)} fusion(bf16[128,256,64]{1,2,0:T(8,128)(2,1)} %bitcast.219, s32[1024]{0:T(1024)S(1)} %pad_clamp_fusion.1), kind=kCustom, calls=%fused_computation.8 | custom fusion | bytes 1048640 | tf_op jit(solution)/shard_map/jit(_take)/gather | solution.py:79
  293.5 3.6 %gather_fusion.9 = bf16[16,256,64]{1,2,0:T(8,128)(2,1)} fusion(bf16[128,256,64]{1,2,0:T(8,128)(2,1)} %bitcast.241, s32[1024]{0:T(1024)S(1)} %pad_clamp_fusion), kind=kCustom, calls=%fused_computation.9 | custom fusion | bytes 1048640 | tf_op jit(solution)/shard_map/jit(_take)/gather | solution.py:80
  308.7 3.2 collective-permute-start.62
  320.3 3.6 %gather_fusion.11 = bf16[16,256,64]{1,2,0:T(8,128)(2,1)} fusion(bf16[128,256,64]{1,2,0:T(8,128)(2,1)} %bitcast.110, s32[1024]{0:T(1024)S(1)} %pad_clamp_fusion), kind=kCustom, calls=%fused_computation.11 | custom fusion | bytes 1048640 | tf_op jit(solution)/shard_map/jit(_take)/gather | solution.py:80
  325.2 3.4 %pad_maximum_fusion.2 = bf16[4,8,2,2,256,64]{4,5,3,2,1,0:T(8,128)(2,1)} fusion(bf16[1,8,2,2,256,64]{4,5,3,2,1,0:T(8,128)(2,1)S(1)} %bitcast.222, bf16[1,8,2,2,256,64]{4,5,3,2,1,0:T(8,128)(2,1)S(1)} %maximum_bitcast_fusion.2, bf16[1,8,2,2,256,64]{4,5,3,2,1,0:T(8,128)(2,1)S(1)} %bitcast.224, bf16[1,8,2,2,256,64]{4,5,3,2,1,0:T(8,128)(2,1)} %bitcast.92), kind=kLoop, calls=%fused_computation.14 | loop fusion | flops 6291456 | bytes 8388608 | tf_op jit(solution)/shard_map/stack | solution.py:31
  331.4 3.0 fusion.39
  (319 shorter events, 190.1 us)
Async XLA Ops:
  2.1 12.8 %all-to-all-start = ((bf16[512,4,128]{0,2,1:T(8,128)(2,1)}), bf16[512,4,128]{0,2,1:T(8,128)(2,1)S(1)}, u32[]{:S(2)}, u32[]{:S(2)}) async-start(bf16[512,4,128]{0,2,1:T(8,128)(2,1)} %bitcast), calls=%async_computation | async-start | bytes 1048576 | tf_op jit(solution)/shard_map/all_to_all | solution.py:46
  18.6 15.6 %collective-permute-start.1 = (bf16[2,2,256,64]{2,3,1,0:T(8,128)(2,1)S(1)}, bf16[2,2,256,64]{2,3,1,0:T(8,128)(2,1)S(1)}, u32[]{:S(2)}, u32[]{:S(2)}) collective-permute-start(bf16[2,2,256,64]{2,3,1,0:T(8,128)(2,1)S(1)} %get-tuple-element.15), channel_id=1, source_target_pairs={{0,56},{8,0},{16,8},{24,16},{32,24},{40,32},{48,40},{56,48},{1,57}... | collective-permute-start | bytes 393224 | tf_op jit(solution)/shard_map/ppermute | solution.py:24
  24.6 12.7 %collective-permute-start.4 = (bf16[2,2,256,64]{2,3,1,0:T(8,128)(2,1)S(1)}, bf16[2,2,256,64]{2,3,1,0:T(8,128)(2,1)S(1)}, u32[]{:S(2)}, u32[]{:S(2)}) collective-permute-start(bf16[2,2,256,64]{2,3,1,0:T(8,128)(2,1)S(1)} %get-tuple-element.15), channel_id=1, source_target_pairs={{0,8},{8,16},{16,24},{24,32},{32,40},{40,48},{48,56},{56,0},{1,9},... | collective-permute-start | bytes 393224 | tf_op jit(solution)/shard_map/ppermute | solution.py:22
  39.8 24.4 %collective-permute-start.17 = (bf16[4,2,2,256,64]{3,4,2,1,0:T(8,128)(2,1)S(1)}, bf16[4,2,2,256,64]{3,4,2,1,0:T(8,128)(2,1)S(1)}, u32[]{:S(2)}, u32[]{:S(2)}) collective-permute-start(bf16[4,2,2,256,64]{3,4,2,1,0:T(8,128)(2,1)S(1)} %pad_maximum_fusion.3), channel_id=1, source_target_pairs={{0,56},{8,0},{16,8},{24,16},{32,24},{40,32},{48,40},{56,48},{1,57}... | collective-permute-start | bytes 1572872 | tf_op jit(solution)/shard_map/ppermute | solution.py:24
  42.9 21.5 %collective-permute-start.20 = (bf16[4,2,2,256,64]{3,4,2,1,0:T(8,128)(2,1)S(1)}, bf16[4,2,2,256,64]{3,4,2,1,0:T(8,128)(2,1)S(1)}, u32[]{:S(2)}, u32[]{:S(2)}) collective-permute-start(bf16[4,2,2,256,64]{3,4,2,1,0:T(8,128)(2,1)S(1)} %pad_maximum_fusion.3), channel_id=1, source_target_pairs={{0,8},{8,16},{16,24},{24,32},{32,40},{40,48},{48,56},{56,0},{1,9},... | collective-permute-start | bytes 1572872 | tf_op jit(solution)/shard_map/ppermute | solution.py:22
  64.3 13.6 %collective-permute-start.18 = (bf16[4,2,2,256,64]{3,4,2,1,0:T(8,128)(2,1)S(1)}, bf16[4,2,2,256,64]{3,4,2,1,0:T(8,128)(2,1)}, u32[]{:S(2)}, u32[]{:S(2)}) collective-permute-start(bf16[4,2,2,256,64]{3,4,2,1,0:T(8,128)(2,1)S(1)} %collective-permute-done.17), channel_id=1, source_target_pairs={{0,56},{8,0},{16,8},{24,16},{32,24},{40,32},{48,40},{56,48},{1,57}... | collective-permute-start | bytes 1572872 | tf_op jit(solution)/shard_map/ppermute | solution.py:24
  64.4 13.5 %collective-permute-start.21 = (bf16[4,2,2,256,64]{3,4,2,1,0:T(8,128)(2,1)S(1)}, bf16[4,2,2,256,64]{3,4,2,1,0:T(8,128)(2,1)}, u32[]{:S(2)}, u32[]{:S(2)}) collective-permute-start(bf16[4,2,2,256,64]{3,4,2,1,0:T(8,128)(2,1)S(1)} %collective-permute-done.20), channel_id=1, source_target_pairs={{0,8},{8,16},{16,24},{24,32},{32,40},{40,48},{48,56},{56,0},{1,9},... | collective-permute-start | bytes 1572872 | tf_op jit(solution)/shard_map/ppermute | solution.py:22
  66.4 29.8 %collective-permute-start.10 = (bf16[8,2,2,256,64]{3,4,2,1,0:T(8,128)(2,1)S(1)}, bf16[8,2,2,256,64]{3,4,2,1,0:T(8,128)(2,1)S(1)}, u32[]{:S(2)}, u32[]{:S(2)}) collective-permute-start(bf16[8,2,2,256,64]{3,4,2,1,0:T(8,128)(2,1)S(1)} %bitcast_dynamic-update-slice_fusion.35), channel_id=1, source_target_pairs={{0,64},{64,128},{128,192},{192,0},{1,65},{65,129},{129,193},{193,1... | collective-permute-start | bytes 3145736 | tf_op jit(solution)/shard_map/ppermute | solution.py:22
  66.5 30.6 %collective-permute-start.9 = (bf16[8,2,2,256,64]{3,4,2,1,0:T(8,128)(2,1)S(1)}, bf16[8,2,2,256,64]{3,4,2,1,0:T(8,128)(2,1)S(1)}, u32[]{:S(2)}, u32[]{:S(2)}) collective-permute-start(bf16[8,2,2,256,64]{3,4,2,1,0:T(8,128)(2,1)S(1)} %bitcast_dynamic-update-slice_fusion.35), channel_id=1, source_target_pairs={{0,192},{64,0},{128,64},{192,128},{1,193},{65,1},{129,65},{193,129... | collective-permute-start | bytes 3145736 | tf_op jit(solution)/shard_map/ppermute | solution.py:24
  77.9 14.6 %collective-permute-start.22 = (bf16[4,2,2,256,64]{3,4,2,1,0:T(8,128)(2,1)}, bf16[4,2,2,256,64]{3,4,2,1,0:T(8,128)(2,1)}, u32[]{:S(2)}, u32[]{:S(2)}) collective-permute-start(bf16[4,2,2,256,64]{3,4,2,1,0:T(8,128)(2,1)} %collective-permute-done.21), channel_id=1, source_target_pairs={{0,8},{8,16},{16,24},{24,32},{32,40},{40,48},{48,56},{56,0},{1,9},... | collective-permute-start | bytes 1572872 | tf_op jit(solution)/shard_map/ppermute | solution.py:22
  97.1 14.2 %collective-permute-start.11 = (bf16[4,2,2,256,64]{3,4,2,1,0:T(8,128)(2,1)}, bf16[4,2,2,256,64]{3,4,2,1,0:T(8,128)(2,1)}, u32[]{:S(2)}, u32[]{:S(2)}) collective-permute-start(bf16[4,2,2,256,64]{3,4,2,1,0:T(8,128)(2,1)} %slice.248), channel_id=1, source_target_pairs={{0,64},{64,128},{128,192},{192,0},{1,65},{65,129},{129,193},{193,1... | collective-permute-start | bytes 1572872 | tf_op jit(solution)/shard_map/ppermute | solution.py:28
  97.9 13.4 %collective-permute-start.12 = (bf16[4,2,2,256,64]{3,4,2,1,0:T(8,128)(2,1)}, bf16[4,2,2,256,64]{3,4,2,1,0:T(8,128)(2,1)}, u32[]{:S(2)}, u32[]{:S(2)}) collective-permute-start(bf16[4,2,2,256,64]{3,4,2,1,0:T(8,128)(2,1)} %slice.249), channel_id=1, source_target_pairs={{0,192},{64,0},{128,64},{192,128},{1,193},{65,1},{129,65},{193,129... | collective-permute-start | bytes 1572872 | tf_op jit(solution)/shard_map/ppermute | solution.py:29
  122.9 18.5 %collective-permute-start.26 = (bf16[2,2,256,64]{2,3,1,0:T(8,128)(2,1)S(1)}, bf16[2,2,256,64]{2,3,1,0:T(8,128)(2,1)S(1)}, u32[]{:S(2)}, u32[]{:S(2)}) collective-permute-start(bf16[2,2,256,64]{2,3,1,0:T(8,128)(2,1)S(1)} %get-tuple-element.12), channel_id=1, source_target_pairs={{0,56},{8,0},{16,8},{24,16},{32,24},{40,32},{48,40},{56,48},{1,57}... | collective-permute-start | bytes 393224 | tf_op jit(solution)/shard_map/ppermute | solution.py:24
  125.4 19.0 %collective-permute-start.29 = (bf16[2,2,256,64]{2,3,1,0:T(8,128)(2,1)S(1)}, bf16[2,2,256,64]{2,3,1,0:T(8,128)(2,1)S(1)}, u32[]{:S(2)}, u32[]{:S(2)}) collective-permute-start(bf16[2,2,256,64]{2,3,1,0:T(8,128)(2,1)S(1)} %get-tuple-element.12), channel_id=1, source_target_pairs={{0,8},{8,16},{16,24},{24,32},{32,40},{40,48},{48,56},{56,0},{1,9},... | collective-permute-start | bytes 393224 | tf_op jit(solution)/shard_map/ppermute | solution.py:22
  125.4 13.8 %collective-permute-start.38 = (bf16[2,2,256,64]{2,3,1,0:T(8,128)(2,1)S(1)}, bf16[2,2,256,64]{2,3,1,0:T(8,128)(2,1)S(1)}, u32[]{:S(2)}, u32[]{:S(2)}) collective-permute-start(bf16[2,2,256,64]{2,3,1,0:T(8,128)(2,1)S(1)} %get-tuple-element.14), channel_id=1, source_target_pairs={{0,192},{64,0},{128,64},{192,128},{1,193},{65,1},{129,65},{193,129... | collective-permute-start | bytes 393224 | tf_op jit(solution)/shard_map/ppermute | solution.py:24
  146.8 29.3 %collective-permute-start.42 = (bf16[4,2,2,256,64]{3,4,2,1,0:T(8,128)(2,1)S(1)}, bf16[4,2,2,256,64]{3,4,2,1,0:T(8,128)(2,1)}, u32[]{:S(2)}, u32[]{:S(2)}) collective-permute-start(bf16[4,2,2,256,64]{3,4,2,1,0:T(8,128)(2,1)S(1)} %pad_maximum_fusion.4), channel_id=1, source_target_pairs={{0,56},{8,0},{16,8},{24,16},{32,24},{40,32},{48,40},{56,48},{1,57}... | collective-permute-start | bytes 1572872 | tf_op jit(solution)/shard_map/ppermute | solution.py:24
  149.8 26.3 %collective-permute-start.45 = (bf16[4,2,2,256,64]{3,4,2,1,0:T(8,128)(2,1)S(1)}, bf16[4,2,2,256,64]{3,4,2,1,0:T(8,128)(2,1)}, u32[]{:S(2)}, u32[]{:S(2)}) collective-permute-start(bf16[4,2,2,256,64]{3,4,2,1,0:T(8,128)(2,1)S(1)} %pad_maximum_fusion.4), channel_id=1, source_target_pairs={{0,8},{8,16},{16,24},{24,32},{32,40},{40,48},{48,56},{56,0},{1,9},... | collective-permute-start | bytes 1572872 | tf_op jit(solution)/shard_map/ppermute | solution.py:22
  172.8 23.4 %collective-permute-start.35 = (bf16[8,2,2,256,64]{3,4,2,1,0:T(8,128)(2,1)}, bf16[8,2,2,256,64]{3,4,2,1,0:T(8,128)(2,1)S(1)}, u32[]{:S(2)}, u32[]{:S(2)}) collective-permute-start(bf16[8,2,2,256,64]{3,4,2,1,0:T(8,128)(2,1)} %bitcast_dynamic-update-slice_fusion.28), channel_id=1, source_target_pairs={{0,64},{64,128},{128,192},{192,0},{1,65},{65,129},{129,193},{193,1... | collective-permute-start | bytes 3145736 | tf_op jit(solution)/shard_map/ppermute | solution.py:22
  172.9 23.5 %collective-permute-start.34 = (bf16[8,2,2,256,64]{3,4,2,1,0:T(8,128)(2,1)}, bf16[8,2,2,256,64]{3,4,2,1,0:T(8,128)(2,1)S(1)}, u32[]{:S(2)}, u32[]{:S(2)}) collective-permute-start(bf16[8,2,2,256,64]{3,4,2,1,0:T(8,128)(2,1)} %bitcast_dynamic-update-slice_fusion.28), channel_id=1, source_target_pairs={{0,192},{64,0},{128,64},{192,128},{1,193},{65,1},{129,65},{193,129... | collective-permute-start | bytes 3145736 | tf_op jit(solution)/shard_map/ppermute | solution.py:24
  187.8 14.1 %collective-permute-start.44 = (bf16[4,2,2,256,64]{3,4,2,1,0:T(8,128)(2,1)}, bf16[4,2,2,256,64]{3,4,2,1,0:T(8,128)(2,1)S(1)}, u32[]{:S(2)}, u32[]{:S(2)}) collective-permute-start(bf16[4,2,2,256,64]{3,4,2,1,0:T(8,128)(2,1)} %collective-permute-done.43), channel_id=1, source_target_pairs={{0,56},{8,0},{16,8},{24,16},{32,24},{40,32},{48,40},{56,48},{1,57}... | collective-permute-start | bytes 1572872 | tf_op jit(solution)/shard_map/ppermute | solution.py:24
  188.2 13.8 %collective-permute-start.47 = (bf16[4,2,2,256,64]{3,4,2,1,0:T(8,128)(2,1)}, bf16[4,2,2,256,64]{3,4,2,1,0:T(8,128)(2,1)S(1)}, u32[]{:S(2)}, u32[]{:S(2)}) collective-permute-start(bf16[4,2,2,256,64]{3,4,2,1,0:T(8,128)(2,1)} %collective-permute-done.46), channel_id=1, source_target_pairs={{0,8},{8,16},{16,24},{24,32},{32,40},{40,48},{48,56},{56,0},{1,9},... | collective-permute-start | bytes 1572872 | tf_op jit(solution)/shard_map/ppermute | solution.py:22
  245.0 24.0 %collective-permute-start.67 = (bf16[4,2,2,256,64]{3,4,2,1,0:T(8,128)(2,1)S(1)}, bf16[4,2,2,256,64]{3,4,2,1,0:T(8,128)(2,1)}, u32[]{:S(2)}, u32[]{:S(2)}) collective-permute-start(bf16[4,2,2,256,64]{3,4,2,1,0:T(8,128)(2,1)S(1)} %pad_maximum_fusion.5), channel_id=1, source_target_pairs={{0,56},{8,0},{16,8},{24,16},{32,24},{40,32},{48,40},{56,48},{1,57}... | collective-permute-start | bytes 1572872 | tf_op jit(solution)/shard_map/ppermute | solution.py:24
  246.6 22.3 %collective-permute-start.70 = (bf16[4,2,2,256,64]{3,4,2,1,0:T(8,128)(2,1)S(1)}, bf16[4,2,2,256,64]{3,4,2,1,0:T(8,128)(2,1)}, u32[]{:S(2)}, u32[]{:S(2)}) collective-permute-start(bf16[4,2,2,256,64]{3,4,2,1,0:T(8,128)(2,1)S(1)} %pad_maximum_fusion.5), channel_id=1, source_target_pairs={{0,8},{8,16},{16,24},{24,32},{32,40},{40,48},{48,56},{56,0},{1,9},... | collective-permute-start | bytes 1572872 | tf_op jit(solution)/shard_map/ppermute | solution.py:22
  247.1 12.6 %collective-permute-start.53 = (bf16[2,2,256,64]{2,3,1,0:T(8,128)(2,1)S(1)}, bf16[2,2,256,64]{2,3,1,0:T(8,128)(2,1)S(1)}, u32[]{:S(2)}, u32[]{:S(2)}) collective-permute-start(bf16[2,2,256,64]{2,3,1,0:T(8,128)(2,1)S(1)} %collective-permute-done.52), channel_id=1, source_target_pairs={{0,56},{8,0},{16,8},{24,16},{32,24},{40,32},{48,40},{56,48},{1,57}... | collective-permute-start | bytes 393224 | tf_op jit(solution)/shard_map/ppermute | solution.py:24
  268.9 12.3 %collective-permute-start.68 = (bf16[4,2,2,256,64]{3,4,2,1,0:T(8,128)(2,1)}, bf16[4,2,2,256,64]{3,4,2,1,0:T(8,128)(2,1)}, u32[]{:S(2)}, u32[]{:S(2)}) collective-permute-start(bf16[4,2,2,256,64]{3,4,2,1,0:T(8,128)(2,1)} %collective-permute-done.67), channel_id=1, source_target_pairs={{0,56},{8,0},{16,8},{24,16},{32,24},{40,32},{48,40},{56,48},{1,57}... | collective-permute-start | bytes 1572872 | tf_op jit(solution)/shard_map/ppermute | solution.py:24
  268.9 12.3 %collective-permute-start.71 = (bf16[4,2,2,256,64]{3,4,2,1,0:T(8,128)(2,1)}, bf16[4,2,2,256,64]{3,4,2,1,0:T(8,128)(2,1)}, u32[]{:S(2)}, u32[]{:S(2)}) collective-permute-start(bf16[4,2,2,256,64]{3,4,2,1,0:T(8,128)(2,1)} %collective-permute-done.70), channel_id=1, source_target_pairs={{0,8},{8,16},{16,24},{24,32},{32,40},{40,48},{48,56},{56,0},{1,9},... | collective-permute-start | bytes 1572872 | tf_op jit(solution)/shard_map/ppermute | solution.py:22
  272.3 34.5 %collective-permute-start.60 = (bf16[8,2,2,256,64]{3,4,2,1,0:T(8,128)(2,1)}, bf16[8,2,2,256,64]{3,4,2,1,0:T(8,128)(2,1)S(1)}, u32[]{:S(2)}, u32[]{:S(2)}) collective-permute-start(bf16[8,2,2,256,64]{3,4,2,1,0:T(8,128)(2,1)} %bitcast_dynamic-update-slice_fusion.21), channel_id=1, source_target_pairs={{0,64},{64,128},{128,192},{192,0},{1,65},{65,129},{129,193},{193,1... | collective-permute-start | bytes 3145736 | tf_op jit(solution)/shard_map/ppermute | solution.py:22
  272.3 35.6 %collective-permute-start.59 = (bf16[8,2,2,256,64]{3,4,2,1,0:T(8,128)(2,1)}, bf16[8,2,2,256,64]{3,4,2,1,0:T(8,128)(2,1)S(1)}, u32[]{:S(2)}, u32[]{:S(2)}) collective-permute-start(bf16[8,2,2,256,64]{3,4,2,1,0:T(8,128)(2,1)} %bitcast_dynamic-update-slice_fusion.21), channel_id=1, source_target_pairs={{0,192},{64,0},{128,64},{192,128},{1,193},{65,1},{129,65},{193,129... | collective-permute-start | bytes 3145736 | tf_op jit(solution)/shard_map/ppermute | solution.py:24
  281.3 19.5 %collective-permute-start.69 = (bf16[4,2,2,256,64]{3,4,2,1,0:T(8,128)(2,1)}, bf16[4,2,2,256,64]{3,4,2,1,0:T(8,128)(2,1)}, u32[]{:S(2)}, u32[]{:S(2)}) collective-permute-start(bf16[4,2,2,256,64]{3,4,2,1,0:T(8,128)(2,1)} %collective-permute-done.68), channel_id=1, source_target_pairs={{0,56},{8,0},{16,8},{24,16},{32,24},{40,32},{48,40},{56,48},{1,57}... | collective-permute-start | bytes 1572872 | tf_op jit(solution)/shard_map/ppermute | solution.py:24
  281.3 21.8 %collective-permute-start.72 = (bf16[4,2,2,256,64]{3,4,2,1,0:T(8,128)(2,1)}, bf16[4,2,2,256,64]{3,4,2,1,0:T(8,128)(2,1)}, u32[]{:S(2)}, u32[]{:S(2)}) collective-permute-start(bf16[4,2,2,256,64]{3,4,2,1,0:T(8,128)(2,1)} %collective-permute-done.71), channel_id=1, source_target_pairs={{0,8},{8,16},{16,24},{24,32},{32,40},{40,48},{48,56},{56,0},{1,9},... | collective-permute-start | bytes 1572872 | tf_op jit(solution)/shard_map/ppermute | solution.py:22
  307.7 16.2 %collective-permute-start.61 = (bf16[4,2,2,256,64]{3,4,2,1,0:T(8,128)(2,1)}, bf16[4,2,2,256,64]{3,4,2,1,0:T(8,128)(2,1)}, u32[]{:S(2)}, u32[]{:S(2)}) collective-permute-start(bf16[4,2,2,256,64]{3,4,2,1,0:T(8,128)(2,1)} %slice.270), channel_id=1, source_target_pairs={{0,64},{64,128},{128,192},{192,0},{1,65},{65,129},{129,193},{193,1... | collective-permute-start | bytes 1572872 | tf_op jit(solution)/shard_map/ppermute | solution.py:28
  308.7 15.2 %collective-permute-start.62 = (bf16[4,2,2,256,64]{3,4,2,1,0:T(8,128)(2,1)}, bf16[4,2,2,256,64]{3,4,2,1,0:T(8,128)(2,1)}, u32[]{:S(2)}, u32[]{:S(2)}) collective-permute-start(bf16[4,2,2,256,64]{3,4,2,1,0:T(8,128)(2,1)} %slice.271), channel_id=1, source_target_pairs={{0,192},{64,0},{128,64},{192,128},{1,193},{65,1},{129,65},{193,129... | collective-permute-start | bytes 1572872 | tf_op jit(solution)/shard_map/ppermute | solution.py:29
  (77 other events, 1200.8 us)

commit v2 on v0

v2 whole, which is shorter than its diff:
```python
import jax
import jax.numpy as jnp
from jax import lax
from jax.experimental import pallas as pl
from jax.experimental.pallas import tpu as pltpu
from jax.sharding import PartitionSpec as P

LEV = 4


def level_solve(table, factor, right, dinv, sources, slot_count):
    per_level, _, block, _ = factor.shape
    width = right.shape[-1]
    n_src = len(sources)
    total = per_level * slot_count

    def kernel(table_ref, f_ref, r_ref, d_ref, *rest):
        src = rest[:n_src]
        o_ref, xs, acc, sem = rest[n_src:]
        b = pl.program_id(0)
        slots = []
        for k in range(slot_count):
            idx = table_ref[0 * total + b * slot_count + k]
            lv = table_ref[1 * total + b * slot_count + k]
            act = table_ref[2 * total + b * slot_count + k]
            slots.append((idx, lv, act))
            for level in range(n_src):
                @pl.when((act > 0) & (lv == level))
                def _():
                    pltpu.make_async_copy(src[level].at[idx], xs.at[k], sem.at[k]).start()
        acc[...] = jnp.zeros_like(acc)
        for k in range(slot_count):
            idx, lv, act = slots[k]

            @pl.when((act > 0) & (lv >= 0) & (lv < n_src))
            def _():
                pltpu.make_async_copy(src[0].at[0], xs.at[k], sem.at[k]).wait()
                acc[...] += jnp.dot(f_ref[0, k], xs[k], preferred_element_type=jnp.float32)

        residual = (r_ref[0].astype(jnp.float32) - acc[...]).astype(jnp.bfloat16)
        o_ref[0] = jnp.dot(d_ref[0], residual, preferred_element_type=jnp.float32).astype(o_ref.dtype)

    any_spec = pl.BlockSpec(memory_space=pl.ANY)
    grid_spec = pltpu.PrefetchScalarGridSpec(
        num_scalar_prefetch=1,
        grid=(per_level,),
        in_specs=[
            pl.BlockSpec((1, slot_count, block, block), lambda b, t: (b, 0, 0, 0)),
            pl.BlockSpec((1, block, width), lambda b, t: (b, 0, 0)),
            pl.BlockSpec((1, block, block), lambda b, t: (b, 0, 0)),
        ]
        + [any_spec] * n_src,
        out_specs=pl.BlockSpec((1, block, width), lambda b, t: (b, 0, 0)),
        scratch_shapes=[
            pltpu.VMEM((slot_count, block, width), sources[0].dtype),
            pltpu.VMEM((block, width), jnp.float32),
            pltpu.SemaphoreType.DMA((slot_count,)),
        ],
    )
    return pl.pallas_call(
        kernel,
        grid_spec=grid_spec,
        out_shape=jax.ShapeDtypeStruct((per_level, block, width), jnp.bfloat16),
    )(table, factor, right, dinv, *sources)


def shards(kernel_rows, factor_blocks, diag_inverse, pattern, live_counts):
    received = lax.all_to_all(kernel_rows, "rhs", split_axis=1, concat_axis=0, tiled=True)
    per_device = factor_blocks.shape[0]
    slot_count = factor_blocks.shape[1]
    block = factor_blocks.shape[2]
    width = received.shape[1]
    right_side = received.reshape(per_device, block, width)
    holders = lax.axis_size("rows")
    per_level = per_device // LEV
    level_of = pattern % per_device // per_level
    holder_of = pattern // per_device
    offset_of = pattern % per_level
    active = jnp.arange(slot_count)[None, :] < live_counts[:, None]
    position = jnp.clip(holder_of * per_level + offset_of, 0, holders * per_level - 1)
    gathered_all = []
    solved_all = []
    for level_now in range(LEV):
        lower = level_now * per_level
        upper = lower + per_level
        if level_now == 0:
            solved = jnp.einsum(
                "bij,bjr->bir", diag_inverse[lower:upper], right_side[lower:upper],
                preferred_element_type=jnp.float32,
            ).astype(jnp.bfloat16)
        else:
            table = jnp.stack(
                [position[lower:upper], level_of[lower:upper], active[lower:upper].astype(jnp.int32)]
            ).reshape(-1).astype(jnp.int32)
            solved = level_solve(
                table,
                factor_blocks[lower:upper],
                right_side[lower:upper],
                diag_inverse[lower:upper],
                gathered_all,
                slot_count,
            )
        solved_all.append(solved)
        if level_now + 1 < LEV:
            gathered_all.append(lax.all_gather(solved, "rows", axis=0, tiled=True))
    return jnp.concatenate(solved_all, axis=0).reshape(per_device * block, width)


def solution(mesh):
    placed = (
        P(("rows", "rhs"), None),
        P("rows", None, None, None),
        P("rows", None, None),
        P("rows", None),
        P("rows"),
    )
    return jax.shard_map(
        shards, mesh=mesh, in_specs=placed, out_specs=P("rows", "rhs"), check_vma=False
    )
```

time: 340 us -> 299 us (0.88)
  other arithmetic: 34 us -> 1.88 us
  Pallas kernels: 0 us -> 19.9 us
  local copies, waits for them, and re-layouts: 25 us -> 10.3 us
  matrix products: 11 us -> 0.88 us
  waiting for transfers between devices: 242 us -> 238 us
    concatenate x2 -> x0, other arithmetic: 31.6 us -> none  [shards(): available = jnp.concatenate(gathered_all, axis=0)]
    gather x6 -> x0, local copies, waits for them, and re-layouts: 21.2 us -> none  [shards(): picked = jnp.take(available, flat_index[lower:upper], axis=0, mode='clip')]
    pallas_call x0 -> x3, Pallas kernels: none -> 19.9 us  [level_solve(): pl.pallas_call(kernel, grid_spec=grid_spec, out_shape=jax.ShapeDtypeStruc...]
    dot_general x4 -> x1, matrix products: 11 us -> 0.88 us  [shards(): jnp.einsum('bij,bjr->bir', diag_inverse[lower:upper], right_side[lower:up...]
    slice x3, local copies, waits for them, and re-layouts: 0.13 us -> 7.36 us  [the longest x1 5.71 us: shards(): factor_blocks[lower:upper]]
    all_gather x3, waiting for transfers between devices: 242 us -> 238 us  [shards(): gathered_all.append(lax.all_gather(solved, 'rows', axis=0, tiled=True))]
  transfers between devices with their start and end apart: 3 -> 3, of which waited for: 3 -> 3; matrix products, arithmetic and copies ran while one was open for 1% -> 3% of each run, Pallas kernels for 0% -> 0%
where the time goes in v2:
time: 299 us; the launch traced here: 297 us
  waiting for transfers between devices  238 us (80%)
  Pallas kernels  19.9 us (7%)
  between operations  13.2 us (4%)
  blocking collectives  12.6 us (4%)
  local copies, waits for them, and re-layouts  10.3 us (3%)
    all_gather x3, waiting for transfers between devices, shards(): gathered_all.append(lax.all_gather(solved, 'rows', axis=0, tiled=True))  238 us
    pallas_call x3, Pallas kernels, level_solve(): pl.pallas_call(kernel, grid_spec=grid_spec, out_shape=jax.ShapeDtypeStruc...  19.9 us
    all_to_all x1, blocking collectives, shards(): lax.all_to_all(kernel_rows, 'rhs', split_axis=1, concat_axis=0, tiled=True)  12.6 us
  transfers between devices with their start and end apart: 3, of which 3 were waited for; matrix products, arithmetic and copies ran while one was open for 3% of the time, Pallas kernels for 0%

profile of v2, /device:TPU:2, one launch (start us, length us, event | category | flops | bytes accessed | tf_op | source)
XLA Modules:
  0.0 296.9 jit_solution(63442371755134304)
XLA Ops:
  6.5 0.0 copy-start
  6.5 0.0 copy-start.1
  6.5 0.0 all-gather.4.cloned.1.call-start
  6.6 1.0 copy-done
  7.6 0.1 copy_bitcast_fusion
  7.7 12.6 %all_to_all.16 = bf16[512,4,128]{2,0,1:T(8,128)(2,1)S(1)} all-to-all(bf16[512,4,128]{2,0,1:T(8,128)(2,1)S(1)} %copy_bitcast_fusion), channel_id=1, replica_groups=mesh['rows'=64,'rhs'=4] {'rhs'}, dimensions={1} | all-to-all | bytes 1048576 | tf_op jit(solution)/shard_map/all_to_all | solution.py:68
  20.3 0.8 fusion.13
  21.1 0.0 copy-done.1
  21.1 0.9 convolution_convert_fusion
  22.0 0.0 all-gather.4.cloned.1.call-update
  22.0 0.0 all-gather.6.cloned.1.call-start
  22.0 0.0 copy-done.6
  22.1 0.1 iota_compare_fusion
  22.1 0.0 copy-done.5
  22.2 0.6 reshape.22.table_ref
  22.8 0.9 fusion.12
  23.7 5.7 %fusion.11 = (bf16[2,8,256,256]{3,2,1,0:T(8,128)(2,1)}, bf16[2,8,256,256]{3,2,1,0:T(8,128)(2,1)}, bf16[2,8,256,256]{3,2,1,0:T(8,128)(2,1)}) fusion(bf16[8,8,256,256]{3,2,1,0:T(8,128)(2,1)} %param.6), kind=kLoop, calls=%fused_computation.40 | loop fusion | bytes 12582912 | tf_op jit(solution)/shard_map/slice | solution.py:97
  29.4 77.8 %all-gather.4.cloned.1.call-done.rest_0_ = bf16[128,256,128]{2,1,0:T(8,128)(2,1)} async-done(((bf16[2,256,128]{2,1,0:T(8,128)(2,1)}), bf16[128,256,128]{2,1,0:T(8,128)(2,1)}) %all-gather.4.cloned.1.call-update) | async-done | bytes 8388624 | tf_op jit(solution)/shard_map/all_gather | solution.py:105
  107.2 7.4 %shard_map.55 = bf16[2,256,128]{2,1,0:T(8,128)(2,1)} custom-call(s32[48]{0:T(128)} %reshape.22.table_ref, bf16[2,8,256,256]{3,2,1,0:T(8,128)(2,1)} %get-tuple-element.6.f_ref, bf16[2,256,128]{2,1,0:T(8,128)(2,1)} %bitcast.34, bf16[2,256,256]{2,1,0:T(8,128)(2,1)} %get-tuple-element.9.d_ref, bf16[128,256,128]{2,1,0:T(8,128)(2,1)} %all-gather.4.cloned.1.call-done.rest_0_), custom_call_target="tpu_custom_call" | custom-call | tf_op jit(solution)/shard_map/pallas_call | solution.py:60
  114.7 0.0 all-gather.6.cloned.1.call-update
  114.7 0.0 all-gather.8.cloned.1.call-start
  114.7 0.6 reshape.23.table_ref
  115.4 79.4 %all-gather.6.cloned.1.call-done.rest_1_ = bf16[128,256,128]{2,1,0:T(8,128)(2,1)} async-done(((bf16[2,256,128]{2,1,0:T(8,128)(2,1)}), bf16[128,256,128]{2,1,0:T(8,128)(2,1)}) %all-gather.6.cloned.1.call-update) | async-done | bytes 8388624 | tf_op jit(solution)/shard_map/all_gather | solution.py:105
  194.8 6.2 %shard_map.56 = bf16[2,256,128]{2,1,0:T(8,128)(2,1)} custom-call(s32[48]{0:T(128)} %reshape.23.table_ref, bf16[2,8,256,256]{3,2,1,0:T(8,128)(2,1)} %get-tuple-element.5.f_ref, bf16[2,256,128]{2,1,0:T(8,128)(2,1)} %bitcast.33, bf16[2,256,256]{2,1,0:T(8,128)(2,1)} %get-tuple-element.8.d_ref, bf16[128,256,128]{2,1,0:T(8,128)(2,1)} %all-gather.4.cloned.1.call-done.rest_0_, ...), custom_call_target="tpu_custom_call" | custom-call | tf_op jit(solution)/shard_map/pallas_call | solution.py:60
  201.0 0.0 all-gather.8.cloned.1.call-update
  201.1 0.6 reshape.24.table_ref
  201.7 80.7 %all-gather.8.cloned.1.call-done.rest_2_ = bf16[128,256,128]{2,1,0:T(8,128)(2,1)} async-done(((bf16[2,256,128]{2,1,0:T(8,128)(2,1)}), bf16[128,256,128]{2,1,0:T(8,128)(2,1)}) %all-gather.8.cloned.1.call-update) | async-done | bytes 8388624 | tf_op jit(solution)/shard_map/all_gather | solution.py:105
  282.4 6.2 %shard_map.57 = bf16[2,256,128]{2,1,0:T(8,128)(2,1)} custom-call(s32[48]{0:T(128)} %reshape.24.table_ref, bf16[2,8,256,256]{3,2,1,0:T(8,128)(2,1)} %get-tuple-element.7.f_ref, bf16[2,256,128]{2,1,0:T(8,128)(2,1)} %bitcast.32, bf16[2,256,256]{2,1,0:T(8,128)(2,1)} %get-tuple-element.10.d_ref, bf16[128,256,128]{2,1,0:T(8,128)(2,1)} %all-gather.4.cloned.1.call-done.rest_0_, ...), custom_call_target="tpu_custom_call" | custom-call | tf_op jit(solution)/shard_map/pallas_call | solution.py:60
  288.6 0.0 copy-done.2
  288.6 0.0 copy-done.3
  288.6 0.0 copy-done.4
  288.6 1.8 pad_maximum_fusion
  (11 shorter events, 0.1 us)
Async XLA Ops:
  6.5 1.0 copy-start
  6.5 14.5 %copy-start.1 = (bf16[8,256,256]{2,1,0:T(8,128)(2,1)S(1)}, bf16[8,256,256]{2,1,0:T(8,128)(2,1)}, u32[]{:S(2)}) copy-start(bf16[8,256,256]{2,1,0:T(8,128)(2,1)} %param.7) | copy-start | bytes 3145732
  6.5 15.5 %copy-start.6 = (s32[8]{0:T(128)S(1)}, s32[8]{0:T(128)}, u32[]{:S(2)}) copy-start(s32[8]{0:T(128)} %param.9) | copy-start | bytes 100
  6.5 15.6 %copy-start.5 = (s32[8,8]{1,0:T(8,128)S(1)}, s32[8,8]{1,0:T(8,128)}, u32[]{:S(2)}) copy-start(s32[8,8]{1,0:T(8,128)} %param.8) | copy-start | bytes 772
  6.5 100.7 %all-gather.4.cloned.1.call-start = ((), (), s32[]{:S(2)}) async-start(), calls=%async_computation.1 | async-start | bytes 8519680 | tf_op jit(solution)/shard_map/all_gather | solution.py:105
  22.0 172.8 %all-gather.6.cloned.1.call-start = ((), (), s32[]{:S(2)}) async-start(), calls=%async_computation.2 | async-start | bytes 8519680 | tf_op jit(solution)/shard_map/all_gather | solution.py:105
  114.7 167.7 %all-gather.8.cloned.1.call-start = ((), (), s32[]{:S(2)}) async-start(), calls=%async_computation.3 | async-start | bytes 8519680 | tf_op jit(solution)/shard_map/all_gather | solution.py:105
  282.4 6.2 %copy-start.2 = (bf16[2,256,128]{2,1,0:T(8,128)(2,1)S(1)}, bf16[2,256,128]{2,1,0:T(8,128)(2,1)}, u32[]{:S(2)}) copy-start(bf16[2,256,128]{2,1,0:T(8,128)(2,1)} %shard_map.55) | copy-start | bytes 393220
  282.4 6.2 %copy-start.3 = (bf16[2,256,128]{2,1,0:T(8,128)(2,1)S(1)}, bf16[2,256,128]{2,1,0:T(8,128)(2,1)}, u32[]{:S(2)}) copy-start(bf16[2,256,128]{2,1,0:T(8,128)(2,1)} %shard_map.56) | copy-start | bytes 393220
  282.4 6.2 %copy-start.4 = (bf16[2,256,128]{2,1,0:T(8,128)(2,1)S(1)}, bf16[2,256,128]{2,1,0:T(8,128)(2,1)}, u32[]{:S(2)}) copy-start(bf16[2,256,128]{2,1,0:T(8,128)(2,1)} %convolution_convert_fusion) | copy-start | bytes 393220
Sparse Core Ops, SparseCore 0:
  22.1 85.0 all-gather.3
  114.8 79.9 all-gather.5
  201.2 81.1 all-gather.7

commit v3 on v2

--- a/solution.py
+++ b/solution.py
@@ -14,52 +14,62 @@
     n_src = len(sources)
     total = per_level * slot_count
 
-    def kernel(table_ref, f_ref, r_ref, d_ref, *rest):
+    def kernel(table_ref, f_hbm, r_hbm, d_hbm, *rest):
         src = rest[:n_src]
-        o_ref, xs, acc, sem = rest[n_src:]
-        b = pl.program_id(0)
+        o_ref, xs, fs, rs, ds, acc, sem, fsem, rsem = rest[n_src:]
+        rcopy = pltpu.make_async_copy(r_hbm, rs, rsem.at[0])
+        dcopy = pltpu.make_async_copy(d_hbm, ds, rsem.at[1])
         slots = []
-        for k in range(slot_count):
-            idx = table_ref[0 * total + b * slot_count + k]
-            lv = table_ref[1 * total + b * slot_count + k]
-            act = table_ref[2 * total + b * slot_count + k]
-            slots.append((idx, lv, act))
+        for s in range(total):
+            b, k = divmod(s, slot_count)
+            idx = table_ref[0 * total + s]
+            lv = table_ref[1 * total + s]
+            act = table_ref[2 * total + s]
+            used = (act > 0) & (lv >= 0) & (lv < n_src)
+            slots.append((used, b, k))
             for level in range(n_src):
                 @pl.when((act > 0) & (lv == level))
                 def _():
-                    pltpu.make_async_copy(src[level].at[idx], xs.at[k], sem.at[k]).start()
-        acc[...] = jnp.zeros_like(acc)
-        for k in range(slot_count):
-            idx, lv, act = slots[k]
+                    pltpu.make_async_copy(src[level].at[idx], xs.at[s], sem.at[s]).start()
 
-            @pl.when((act > 0) & (lv >= 0) & (lv < n_src))
+            @pl.when(used)
             def _():
-                pltpu.make_async_copy(src[0].at[0], xs.at[k], sem.at[k]).wait()
-                acc[...] += jnp.dot(f_ref[0, k], xs[k], preferred_element_type=jnp.float32)
+                pltpu.make_async_copy(f_hbm.at[b, k], fs.at[s], fsem.at[s]).start()
 
-        residual = (r_ref[0].astype(jnp.float32) - acc[...]).astype(jnp.bfloat16)
-        o_ref[0] = jnp.dot(d_ref[0], residual, preferred_element_type=jnp.float32).astype(o_ref.dtype)
+        rcopy.start()
+        dcopy.start()
+        rcopy.wait()
+        dcopy.wait()
+        for b in range(per_level):
+            acc[...] = jnp.zeros_like(acc)
+            for k in range(slot_count):
+                s = b * slot_count + k
+                used = slots[s][0]
+
+                @pl.when(used)
+                def _():
+                    pltpu.make_async_copy(src[0].at[0], xs.at[s], sem.at[s]).wait()
+                    pltpu.make_async_copy(f_hbm.at[0, 0], fs.at[s], fsem.at[s]).wait()
+                    acc[...] += jnp.dot(fs[s], xs[s], preferred_element_type=jnp.float32)
+
+            residual = (rs[b].astype(jnp.float32) - acc[...]).astype(jnp.bfloat16)
+            o_ref[b] = jnp.dot(ds[b], residual, preferred_element_type=jnp.float32).astype(o_ref.dtype)
 
     any_spec = pl.BlockSpec(memory_space=pl.ANY)
-    grid_spec = pltpu.PrefetchScalarGridSpec(
-        num_scalar_prefetch=1,
-        grid=(per_level,),
-        in_specs=[
-            pl.BlockSpec((1, slot_count, block, block), lambda b, t: (b, 0, 0, 0)),
-            pl.BlockSpec((1, block, width), lambda b, t: (b, 0, 0)),
-            pl.BlockSpec((1, block, block), lambda b, t: (b, 0, 0)),
-        ]
-        + [any_spec] * n_src,
-        out_specs=pl.BlockSpec((1, block, width), lambda b, t: (b, 0, 0)),
-        scratch_shapes=[
-            pltpu.VMEM((slot_count, block, width), sources[0].dtype),
-            pltpu.VMEM((block, width), jnp.float32),
-            pltpu.SemaphoreType.DMA((slot_count,)),
-        ],
-    )
     return pl.pallas_call(
         kernel,
-        grid_spec=grid_spec,
+        in_specs=[pl.BlockSpec(memory_space=pltpu.SMEM), any_spec, any_spec, any_spec] + [any_spec] * n_src,
+        out_specs=pl.BlockSpec(memory_space=pltpu.VMEM),
+        scratch_shapes=[
+            pltpu.VMEM((total, block, width), sources[0].dtype),
+            pltpu.VMEM((total, block, block), factor.dtype),
+            pltpu.VMEM((per_level, block, width), right.dtype),
+            pltpu.VMEM((per_level, block, block), dinv.dtype),
+            pltpu.VMEM((block, width), jnp.float32),
+            pltpu.SemaphoreType.DMA((total,)),
+            pltpu.SemaphoreType.DMA((total,)),
+            pltpu.SemaphoreType.DMA((2,)),
+        ],
         out_shape=jax.ShapeDtypeStruct((per_level, block, width), jnp.bfloat16),
     )(table, factor, right, dinv, *sources)
 

time: 299 us -> 296 us (0.990)
  no operation moved by 1% of the time
where the time goes in v3:
time: 296 us; the launch traced here: 295 us
  waiting for transfers between devices  237 us (80%)
  Pallas kernels  18.7 us (6%)
  between operations  13.2 us (4%)
  blocking collectives  12.6 us (4%)
  local copies, waits for them, and re-layouts  10.3 us (3%)
    all_gather x3, waiting for transfers between devices, shards(): gathered_all.append(lax.all_gather(solved, 'rows', axis=0, tiled=True))  237 us
    pallas_call x3, Pallas kernels, level_solve(): pl.pallas_call(kernel, in_specs=[pl.BlockSpec(memory_space=pltpu.SMEM), a...  18.7 us
    all_to_all x1, blocking collectives, shards(): lax.all_to_all(kernel_rows, 'rhs', split_axis=1, concat_axis=0, tiled=True)  12.6 us
  transfers between devices with their start and end apart: 3, of which 3 were waited for; matrix products, arithmetic and copies ran while one was open for 3% of the time, Pallas kernels for 0%

profile of v3, /device:TPU:2, one launch (start us, length us, event | category | flops | bytes accessed | tf_op | source)
XLA Modules:
  0.0 294.9 jit_solution(11570458654061313958)
XLA Ops:
  6.5 0.0 copy-start
  6.5 0.0 copy-start.1
  6.5 0.0 all-gather.4.cloned.1.call-start
  6.6 1.0 copy-done
  7.6 0.1 copy_bitcast_fusion
  7.7 12.6 %all_to_all.16 = bf16[512,4,128]{2,0,1:T(8,128)(2,1)S(1)} all-to-all(bf16[512,4,128]{2,0,1:T(8,128)(2,1)S(1)} %copy_bitcast_fusion), channel_id=1, replica_groups=mesh['rows'=64,'rhs'=4] {'rhs'}, dimensions={1} | all-to-all | bytes 1048576 | tf_op jit(solution)/shard_map/all_to_all | solution.py:78
  20.3 0.8 fusion.13
  21.1 0.0 copy-done.1
  21.1 0.9 convolution_convert_fusion
  22.0 0.0 all-gather.4.cloned.1.call-update
  22.0 0.0 all-gather.6.cloned.1.call-start
  22.0 0.0 copy-done.6
  22.1 0.1 iota_compare_fusion
  22.1 0.0 copy-done.5
  22.2 0.6 reshape.22.table_ref
  22.8 0.9 fusion.12
  23.7 5.7 %fusion.11 = (bf16[2,8,256,256]{3,2,1,0:T(8,128)(2,1)}, bf16[2,8,256,256]{3,2,1,0:T(8,128)(2,1)}, bf16[2,8,256,256]{3,2,1,0:T(8,128)(2,1)}) fusion(bf16[8,8,256,256]{3,2,1,0:T(8,128)(2,1)} %param.6), kind=kLoop, calls=%fused_computation.40 | loop fusion | bytes 12582912 | tf_op jit(solution)/shard_map/slice | solution.py:107
  29.4 77.8 %all-gather.4.cloned.1.call-done.rest_0_ = bf16[128,256,128]{2,1,0:T(8,128)(2,1)} async-done(((bf16[2,256,128]{2,1,0:T(8,128)(2,1)}), bf16[128,256,128]{2,1,0:T(8,128)(2,1)}) %all-gather.4.cloned.1.call-update) | async-done | bytes 8388624 | tf_op jit(solution)/shard_map/all_gather | solution.py:115
  107.2 6.2 %shard_map.55 = bf16[2,256,128]{2,1,0:T(8,128)(2,1)} custom-call(s32[48]{0:T(128)} %reshape.22.table_ref, bf16[2,8,256,256]{3,2,1,0:T(8,128)(2,1)} %get-tuple-element.6.f_hbm, bf16[2,256,128]{2,1,0:T(8,128)(2,1)} %bitcast.34, bf16[2,256,256]{2,1,0:T(8,128)(2,1)} %get-tuple-element.9.d_hbm, bf16[128,256,128]{2,1,0:T(8,128)(2,1)} %all-gather.4.cloned.1.call-done.rest_0_), custom_call_target="tpu_custom_call" | custom-call | tf_op jit(solution)/shard_map/pallas_call | solution.py:59
  113.4 0.0 all-gather.6.cloned.1.call-update
  113.4 0.0 all-gather.8.cloned.1.call-start
  113.5 0.6 reshape.23.table_ref
  114.1 79.6 %all-gather.6.cloned.1.call-done.rest_1_ = bf16[128,256,128]{2,1,0:T(8,128)(2,1)} async-done(((bf16[2,256,128]{2,1,0:T(8,128)(2,1)}), bf16[128,256,128]{2,1,0:T(8,128)(2,1)}) %all-gather.6.cloned.1.call-update) | async-done | bytes 8388624 | tf_op jit(solution)/shard_map/all_gather | solution.py:115
  193.7 5.9 %shard_map.56 = bf16[2,256,128]{2,1,0:T(8,128)(2,1)} custom-call(s32[48]{0:T(128)} %reshape.23.table_ref, bf16[2,8,256,256]{3,2,1,0:T(8,128)(2,1)} %get-tuple-element.5.f_hbm, bf16[2,256,128]{2,1,0:T(8,128)(2,1)} %bitcast.33, bf16[2,256,256]{2,1,0:T(8,128)(2,1)} %get-tuple-element.8.d_hbm, bf16[128,256,128]{2,1,0:T(8,128)(2,1)} %all-gather.4.cloned.1.call-done.rest_0_, ...), custom_call_target="tpu_custom_call" | custom-call | tf_op jit(solution)/shard_map/pallas_call | solution.py:59
  199.7 0.0 all-gather.8.cloned.1.call-update
  199.7 0.6 reshape.24.table_ref
  200.3 79.8 %all-gather.8.cloned.1.call-done.rest_2_ = bf16[128,256,128]{2,1,0:T(8,128)(2,1)} async-done(((bf16[2,256,128]{2,1,0:T(8,128)(2,1)}), bf16[128,256,128]{2,1,0:T(8,128)(2,1)}) %all-gather.8.cloned.1.call-update) | async-done | bytes 8388624 | tf_op jit(solution)/shard_map/all_gather | solution.py:115
  280.1 6.5 %shard_map.57 = bf16[2,256,128]{2,1,0:T(8,128)(2,1)} custom-call(s32[48]{0:T(128)} %reshape.24.table_ref, bf16[2,8,256,256]{3,2,1,0:T(8,128)(2,1)} %get-tuple-element.7.f_hbm, bf16[2,256,128]{2,1,0:T(8,128)(2,1)} %bitcast.32, bf16[2,256,256]{2,1,0:T(8,128)(2,1)} %get-tuple-element.10.d_hbm, bf16[128,256,128]{2,1,0:T(8,128)(2,1)} %all-gather.4.cloned.1.call-done.rest_0_, ...), custom_call_target="tpu_custom_call" | custom-call | tf_op jit(solution)/shard_map/pallas_call | solution.py:59
  286.6 0.0 copy-done.2
  286.6 0.0 copy-done.3
  286.6 0.0 copy-done.4
  286.6 1.8 pad_maximum_fusion
  (11 shorter events, 0.1 us)
Async XLA Ops:
  6.5 1.0 copy-start
  6.5 14.5 %copy-start.1 = (bf16[8,256,256]{2,1,0:T(8,128)(2,1)S(1)}, bf16[8,256,256]{2,1,0:T(8,128)(2,1)}, u32[]{:S(2)}) copy-start(bf16[8,256,256]{2,1,0:T(8,128)(2,1)} %param.7) | copy-start | bytes 3145732
  6.5 15.5 %copy-start.6 = (s32[8]{0:T(128)S(1)}, s32[8]{0:T(128)}, u32[]{:S(2)}) copy-start(s32[8]{0:T(128)} %param.9) | copy-start | bytes 100
  6.5 15.6 %copy-start.5 = (s32[8,8]{1,0:T(8,128)S(1)}, s32[8,8]{1,0:T(8,128)}, u32[]{:S(2)}) copy-start(s32[8,8]{1,0:T(8,128)} %param.8) | copy-start | bytes 772
  6.5 100.7 %all-gather.4.cloned.1.call-start = ((), (), s32[]{:S(2)}) async-start(), calls=%async_computation.1 | async-start | bytes 8519680 | tf_op jit(solution)/shard_map/all_gather | solution.py:115
  22.0 171.7 %all-gather.6.cloned.1.call-start = ((), (), s32[]{:S(2)}) async-start(), calls=%async_computation.2 | async-start | bytes 8519680 | tf_op jit(solution)/shard_map/all_gather | solution.py:115
  113.4 166.6 %all-gather.8.cloned.1.call-start = ((), (), s32[]{:S(2)}) async-start(), calls=%async_computation.3 | async-start | bytes 8519680 | tf_op jit(solution)/shard_map/all_gather | solution.py:115
  280.1 6.6 %copy-start.2 = (bf16[2,256,128]{2,1,0:T(8,128)(2,1)S(1)}, bf16[2,256,128]{2,1,0:T(8,128)(2,1)}, u32[]{:S(2)}) copy-start(bf16[2,256,128]{2,1,0:T(8,128)(2,1)} %shard_map.55) | copy-start | bytes 393220
  280.1 6.6 %copy-start.3 = (bf16[2,256,128]{2,1,0:T(8,128)(2,1)S(1)}, bf16[2,256,128]{2,1,0:T(8,128)(2,1)}, u32[]{:S(2)}) copy-start(bf16[2,256,128]{2,1,0:T(8,128)(2,1)} %shard_map.56) | copy-start | bytes 393220
  280.1 6.6 %copy-start.4 = (bf16[2,256,128]{2,1,0:T(8,128)(2,1)S(1)}, bf16[2,256,128]{2,1,0:T(8,128)(2,1)}, u32[]{:S(2)}) copy-start(bf16[2,256,128]{2,1,0:T(8,128)(2,1)} %convolution_convert_fusion) | copy-start | bytes 393220
Sparse Core Ops, SparseCore 0:
  22.1 85.0 all-gather.3
  113.5 80.1 all-gather.5
  199.8 80.1 all-gather.7

commit v4 on v1

v4 whole, which is shorter than its diff:
```python
import jax
import jax.numpy as jnp
from jax import lax
from jax.experimental import pallas as pl
from jax.experimental.pallas import tpu as pltpu
from jax.sharding import Mesh
from jax.sharding import PartitionSpec as P

LEV = 4
ROWS = ("y", "z", "core")


def ring(n, step):
    return [(i, (i + step) % n) for i in range(n)]


def ring_pieces(x, axis, n):
    lead = x.shape[0]
    pieces = [(x, 0, 0, lead)]
    fwd = x
    bwd = x
    for k in range(1, (n - 1) // 2 + 1):
        fwd = lax.ppermute(fwd, axis, ring(n, 1))
        pieces.append((fwd, n - k, 0, lead))
        bwd = lax.ppermute(bwd, axis, ring(n, -1))
        pieces.append((bwd, k, 0, lead))
    if n % 2 == 0 and n > 1:
        m = lead // 2
        pieces.append((lax.ppermute(fwd[:m], axis, ring(n, 1)), n // 2, 0, m))
        pieces.append((lax.ppermute(bwd[m:], axis, ring(n, -1)), n // 2, m, lead - m))
    return pieces


def ring_stack(x, axis, n):
    got = [None] * n
    for arr, j, lo, count in ring_pieces(x, axis, n):
        got[j] = arr if got[j] is None else jnp.concatenate([got[j], arr], 0)
    return jnp.stack(got)


def gather_level(solved, ny, nz):
    core = lax.axis_index("core")
    other = lax.ppermute(solved, "core", ring(2, 1))
    chip = jnp.where(core == 0, jnp.stack([solved, other]), jnp.stack([other, solved]))
    out = []
    by_z = ring_stack(chip[:, 0], "z", nz)
    for arr, j, lo, count in ring_pieces(by_z, "y", ny):
        out.append((arr.reshape(-1, *arr.shape[-2:]), 0, j, lo, count))
    by_y = ring_stack(chip[:, 1], "y", ny)
    for arr, j, lo, count in ring_pieces(by_y, "z", nz):
        out.append((arr.reshape(-1, *arr.shape[-2:]), 1, j, lo, count))
    return out


def level_solve(table, factor, right, dinv, sources, slot_count):
    per_level, _, block, _ = factor.shape
    width = right.shape[-1]
    n_src = len(sources)
    total = per_level * slot_count

    def kernel(table_ref, f_hbm, r_hbm, d_hbm, *rest):
        src = rest[:n_src]
        o_ref, xs, fs, rs, ds, acc, sem, fsem, rsem = rest[n_src:]
        rcopy = pltpu.make_async_copy(r_hbm, rs, rsem.at[0])
        dcopy = pltpu.make_async_copy(d_hbm, ds, rsem.at[1])
        slots = []
        for s in range(total):
            b, k = divmod(s, slot_count)
            idx = table_ref[0 * total + s]
            piece = table_ref[1 * total + s]
            act = table_ref[2 * total + s]
            used = (act > 0) & (piece >= 0) & (piece < n_src)
            slots.append((used, b, k))
            for p in range(n_src):
                @pl.when((act > 0) & (piece == p))
                def _():
                    pltpu.make_async_copy(src[p].at[idx], xs.at[s], sem.at[s]).start()

            @pl.when(used)
            def _():
                pltpu.make_async_copy(f_hbm.at[b, k], fs.at[s], fsem.at[s]).start()

        rcopy.start()
        dcopy.start()
        rcopy.wait()
        dcopy.wait()
        for b in range(per_level):
            acc[...] = jnp.zeros_like(acc)
            for k in range(slot_count):
                s = b * slot_count + k
                used = slots[s][0]

                @pl.when(used)
                def _():
                    pltpu.make_async_copy(src[0].at[0], xs.at[s], sem.at[s]).wait()
                    pltpu.make_async_copy(f_hbm.at[0, 0], fs.at[s], fsem.at[s]).wait()
                    acc[...] += jnp.dot(fs[s], xs[s], preferred_element_type=jnp.float32)

            residual = (rs[b].astype(jnp.float32) - acc[...]).astype(jnp.bfloat16)
            o_ref[b] = jnp.dot(ds[b], residual, preferred_element_type=jnp.float32).astype(o_ref.dtype)

    any_spec = pl.BlockSpec(memory_space=pl.ANY)
    return pl.pallas_call(
        kernel,
        in_specs=[pl.BlockSpec(memory_space=pltpu.SMEM), any_spec, any_spec, any_spec] + [any_spec] * n_src,
        out_specs=pl.BlockSpec(memory_space=pltpu.VMEM),
        scratch_shapes=[
            pltpu.VMEM((total, block, width), right.dtype),
            pltpu.VMEM((total, block, block), factor.dtype),
            pltpu.VMEM((per_level, block, width), right.dtype),
            pltpu.VMEM((per_level, block, block), dinv.dtype),
            pltpu.VMEM((block, width), jnp.float32),
            pltpu.SemaphoreType.DMA((total,)),
            pltpu.SemaphoreType.DMA((total,)),
            pltpu.SemaphoreType.DMA((2,)),
        ],
        out_shape=jax.ShapeDtypeStruct((per_level, block, width), jnp.bfloat16),
    )(table, factor, right, dinv, *sources)


def make_shards(ny, nz):
    def shards(kernel_rows, factor_blocks, diag_inverse, pattern, live_counts):
        received = lax.all_to_all(kernel_rows, "x", split_axis=1, concat_axis=0, tiled=True)
        per_device = factor_blocks.shape[0]
        slot_count = factor_blocks.shape[1]
        block = factor_blocks.shape[2]
        width = received.shape[1]
        right_side = received.reshape(per_device, block, width)
        per_level = per_device // LEV
        level_of = pattern % per_device // per_level
        holder_of = pattern // per_device
        offset_of = pattern % per_level
        active = (jnp.arange(slot_count)[None, :] < live_counts[:, None]).astype(jnp.int32)
        hc = holder_of % 2
        jy = (holder_of // (nz * 2) - lax.axis_index("y")) % ny
        jz = (holder_of // 2 % nz - lax.axis_index("z")) % nz
        pieces = []
        solved_all = []
        for level_now in range(LEV):
            lower = level_now * per_level
            upper = lower + per_level
            if level_now == 0:
                solved = jnp.einsum(
                    "bij,bjr->bir", diag_inverse[lower:upper], right_side[lower:upper],
                    preferred_element_type=jnp.float32,
                ).astype(jnp.bfloat16)
            else:
                lv = level_of[lower:upper]
                off = offset_of[lower:upper]
                sy = jy[lower:upper]
                sz = jz[lower:upper]
                sc = hc[lower:upper]
                piece_id = jnp.full(lv.shape, -1, jnp.int32)
                local = jnp.zeros(lv.shape, jnp.int32)
                for p, (source, (arr, kind, j, lo, count)) in enumerate(pieces):
                    main, sub = (sy, sz) if kind == 0 else (sz, sy)
                    match = (lv == source) & (off == kind) & (main == j) & (sub >= lo) & (sub < lo + count)
                    piece_id = jnp.where(match, p, piece_id)
                    local = jnp.where(match, (sub - lo) * 2 + sc, local)
                table = jnp.stack([local, piece_id, active[lower:upper]]).reshape(-1).astype(jnp.int32)
                solved = level_solve(
                    table,
                    factor_blocks[lower:upper],
                    right_side[lower:upper],
                    diag_inverse[lower:upper],
                    [arr for _, (arr, *_rest) in pieces],
                    slot_count,
                )
            solved_all.append(solved)
            if level_now + 1 < LEV:
                pieces += [(level_now, piece) for piece in gather_level(solved, ny, nz)]
        return jnp.concatenate(solved_all, axis=0).reshape(per_device * block, width)

    return shards


def solution(mesh):
    rows = mesh.shape["rows"]
    devices = mesh.devices
    try:
        ny = len({d.coords[1] for d in devices.flat})
        nz = len({d.coords[2] for d in devices.flat})
    except Exception:
        ny, nz = 4, rows // 8
    fine = Mesh(devices.reshape(ny, nz, rows // (ny * nz), mesh.shape["rhs"]), ROWS + ("x",))
    placed = (
        P(ROWS + ("x",), None),
        P(ROWS, None, None, None),
        P(ROWS, None, None),
        P(ROWS, None),
        P(ROWS),
    )
    return jax.shard_map(
        make_shards(ny, nz), mesh=fine, in_specs=placed, out_specs=P(ROWS, "x"), check_vma=False
    )
```

time: 342 us -> 302 us (0.88)
  the two profiles are of different devices: /device:TPU:2 before, /device:TPU:96 now
where the time goes in v4:
time: 302 us; the launch traced here: 297 us
  starting transfers between devices  132 us (44%)
  waiting for transfers between devices  114 us (38%)
  local copies, waits for them, and re-layouts  26 us (9%)
  Pallas kernels  15.4 us (5%)
  other arithmetic  7.66 us (3%)
    ppermute x24, starting transfers between devices, ring_pieces(): fwd = lax.ppermute(fwd, axis, ring(n, 1))  63.3 us
    ppermute x24, waiting for transfers between devices, ring_pieces(): bwd = lax.ppermute(bwd, axis, ring(n, -1))  40.4 us
    ppermute x24, waiting for transfers between devices, ring_pieces(): fwd = lax.ppermute(fwd, axis, ring(n, 1))  29.8 us
    ppermute x24, starting transfers between devices, ring_pieces(): bwd = lax.ppermute(bwd, axis, ring(n, -1))  23.2 us
    ppermute x12, waiting for transfers between devices, ring_pieces(): lax.ppermute(bwd[m:], axis, ring(n, -1))  22.1 us
    ppermute x12, starting transfers between devices, ring_pieces(): lax.ppermute(bwd[m:], axis, ring(n, -1))  21.3 us
    ppermute x12, starting transfers between devices, ring_pieces(): pieces.append((lax.ppermute(fwd[:m], axis, ring(n, 1)), n // 2, 0, m))  19.6 us
    pallas_call x3, Pallas kernels, level_solve(): pl.pallas_call(kernel, in_specs=[pl.BlockSpec(memory_space=pltpu.SMEM), a...  15.4 us
  transfers between devices with their start and end apart: 76, of which 32 were waited for; matrix products, arithmetic and copies ran while one was open for 8% of the time, Pallas kernels for 0%

profile of v4, /device:TPU:96, one launch (start us, length us, event | category | flops | bytes accessed | tf_op | source)
XLA Modules:
  0.0 296.6 jit_solution(13370398375300799522)
XLA Ops:
  1.9 4.3 %all-to-all-start = ((bf16[512,4,128]{2,0,1:T(8,128)(2,1)}), bf16[512,4,128]{2,0,1:T(8,128)(2,1)S(1)}, u32[]{:S(2)}, u32[]{:S(2)}) async-start(bf16[512,4,128]{2,0,1:T(8,128)(2,1)} %copy_bitcast_fusion), calls=%async_computation | async-start | bytes 1048576 | tf_op jit(solution)/shard_map/all_to_all | solution.py:123
  7.5 8.2 %all-to-all-done = bf16[512,4,128]{2,0,1:T(8,128)(2,1)S(1)} async-done(((bf16[512,4,128]{2,0,1:T(8,128)(2,1)}), bf16[512,4,128]{2,0,1:T(8,128)(2,1)S(1)}, u32[]{:S(2)}, u32[]{:S(2)}) %all-to-all-start) | async-done | bytes 524320 | tf_op jit(solution)/shard_map/all_to_all | solution.py:123
  24.8 3.3 %collective-permute-done.13 = bf16[2,256,128]{2,1,0:T(8,128)(2,1)S(1)} collective-permute-done((bf16[2,256,128]{2,1,0:T(8,128)(2,1)S(1)}, bf16[2,256,128]{2,1,0:T(8,128)(2,1)S(1)}, u32[]{:S(2)}, u32[]{:S(2)}) %collective-permute-start.13) | collective-permute-done | bytes 131104 | tf_op jit(solution)/shard_map/ppermute | solution.py:25
  42.1 11.5 %collective-permute-done.3 = bf16[2,256,128]{2,1,0:T(8,128)(2,1)S(1)} collective-permute-done((bf16[2,256,128]{2,1,0:T(8,128)(2,1)S(1)}, bf16[2,256,128]{2,1,0:T(8,128)(2,1)S(1)}, u32[]{:S(2)}, u32[]{:S(2)}) %collective-permute-start.3) | collective-permute-done | bytes 131104 | tf_op jit(solution)/shard_map/ppermute | solution.py:25
  53.6 3.5 %collective-permute-start.7 = (bf16[1,256,128]{2,1,0:T(8,128)(2,1)S(1)}, bf16[1,256,128]{2,1,0:T(8,128)(2,1)S(1)}, u32[]{:S(2)}, u32[]{:S(2)}) collective-permute-start(bf16[1,256,128]{2,1,0:T(8,128)(2,1)S(1)} %slice.255), channel_id=1, source_target_pairs={{0,8},{8,16},{16,24},{24,32},{32,40},{40,48},{48,56},{56,0},{1,9},... | collective-permute-start | bytes 196616 | tf_op jit(solution)/shard_map/ppermute | solution.py:29
  62.5 3.6 %collective-permute-start.19 = (bf16[4,2,256,128]{3,2,1,0:T(8,128)(2,1)S(1)}, bf16[4,2,256,128]{3,2,1,0:T(8,128)(2,1)S(1)}, u32[]{:S(2)}, u32[]{:S(2)}) collective-permute-start(bf16[4,2,256,128]{3,2,1,0:T(8,128)(2,1)S(1)} %collective-permute-done.17), channel_id=1, source_target_pairs={{0,8},{8,16},{16,24},{24,32},{32,40},{40,48},{48,56},{56,0},{1,9},... | collective-permute-start | bytes 1572872 | tf_op jit(solution)/shard_map/ppermute | solution.py:23
  66.8 5.8 %fusion.40 = (bf16[2,8,256,256]{3,2,1,0:T(8,128)(2,1)}, bf16[2,8,256,256]{3,2,1,0:T(8,128)(2,1)}, bf16[2,8,256,256]{3,2,1,0:T(8,128)(2,1)}) fusion(bf16[8,8,256,256]{3,2,1,0:T(8,128)(2,1)} %param.6), kind=kLoop, calls=%fused_computation.285 | loop fusion | bytes 12582912 | tf_op jit(solution)/shard_map/slice | solution.py:163
  72.6 3.5 %collective-permute-done.19 = bf16[4,2,256,128]{3,2,1,0:T(8,128)(2,1)S(1)} collective-permute-done((bf16[4,2,256,128]{3,2,1,0:T(8,128)(2,1)S(1)}, bf16[4,2,256,128]{3,2,1,0:T(8,128)(2,1)S(1)}, u32[]{:S(2)}, u32[]{:S(2)}) %collective-permute-start.19) | collective-permute-done | bytes 524320 | tf_op jit(solution)/shard_map/ppermute | solution.py:23
  76.1 3.7 %collective-permute-start.21 = (bf16[4,2,256,128]{3,2,1,0:T(8,128)(2,1)S(1)}, bf16[4,2,256,128]{3,2,1,0:T(8,128)(2,1)S(1)}, u32[]{:S(2)}, u32[]{:S(2)}) collective-permute-start(bf16[4,2,256,128]{3,2,1,0:T(8,128)(2,1)S(1)} %collective-permute-done.19), channel_id=1, source_target_pairs={{0,8},{8,16},{16,24},{24,32},{32,40},{40,48},{48,56},{56,0},{1,9},... | collective-permute-start | bytes 1572872 | tf_op jit(solution)/shard_map/ppermute | solution.py:23
  90.0 3.7 %collective-permute-start.23 = (bf16[2,2,256,128]{3,2,1,0:T(8,128)(2,1)}, bf16[2,2,256,128]{3,2,1,0:T(8,128)(2,1)S(1)}, u32[]{:S(2)}, u32[]{:S(2)}) collective-permute-start(bf16[2,2,256,128]{3,2,1,0:T(8,128)(2,1)} %slice.262), channel_id=1, source_target_pairs={{0,8},{8,16},{16,24},{24,32},{32,40},{40,48},{48,56},{56,0},{1,9},... | collective-permute-start | bytes 786440 | tf_op jit(solution)/shard_map/ppermute | solution.py:29
  97.9 5.2 %collective-permute-done.24 = bf16[2,2,256,128]{3,2,1,0:T(8,128)(2,1)} collective-permute-done((bf16[2,2,256,128]{3,2,1,0:T(8,128)(2,1)}, bf16[2,2,256,128]{3,2,1,0:T(8,128)(2,1)}, u32[]{:S(2)}, u32[]{:S(2)}) %collective-permute-start.24) | collective-permute-done | bytes 262176 | tf_op jit(solution)/shard_map/ppermute | solution.py:30
  103.2 4.7 %shard_map.55 = bf16[2,256,128]{2,1,0:T(8,128)(2,1)} custom-call(s32[48]{0:T(128)} %reshape.148.table_ref, bf16[2,8,256,256]{3,2,1,0:T(8,128)(2,1)} %get-tuple-element.70.f_hbm, bf16[2,256,128]{2,1,0:T(8,128)(2,1)} %bitcast.230, bf16[2,256,256]{2,1,0:T(8,128)(2,1)} %get-tuple-element.73.d_hbm, bf16[16,256,128]{2,1,0:T(8,128)(2,1)} %bitcast.169, ...), custom_call_target="tpu_custom_call" | custom-call | tf_op jit(solution)/shard_map/pallas_call | solution.py:103
  110.7 11.8 %collective-permute-start.29 = (bf16[2,256,128]{2,1,0:T(8,128)(2,1)S(1)}, bf16[2,256,128]{2,1,0:T(8,128)(2,1)S(1)}, u32[]{:S(2)}, u32[]{:S(2)}) collective-permute-start(bf16[2,256,128]{2,1,0:T(8,128)(2,1)S(1)} %get-tuple-element.83), channel_id=1, source_target_pairs={{0,8},{8,16},{16,24},{24,32},{32,40},{40,48},{48,56},{56,0},{1,9},... | collective-permute-start | bytes 393224 | tf_op jit(solution)/shard_map/ppermute | solution.py:23
  128.3 3.7 %collective-permute-start.41 = (bf16[1,256,128]{2,1,0:T(8,128)(2,1)S(1)}, bf16[1,256,128]{2,1,0:T(8,128)(2,1)S(1)}, u32[]{:S(2)}, u32[]{:S(2)}) collective-permute-start(bf16[1,256,128]{2,1,0:T(8,128)(2,1)S(1)} %slice.272), channel_id=1, source_target_pairs={{0,192},{64,0},{128,64},{192,128},{1,193},{65,1},{129,65},{193,129... | collective-permute-start | bytes 196616 | tf_op jit(solution)/shard_map/ppermute | solution.py:30
  139.8 3.4 %collective-permute-start.31 = (bf16[2,256,128]{2,1,0:T(8,128)(2,1)S(1)}, bf16[2,256,128]{2,1,0:T(8,128)(2,1)S(1)}, u32[]{:S(2)}, u32[]{:S(2)}) collective-permute-start(bf16[2,256,128]{2,1,0:T(8,128)(2,1)S(1)} %collective-permute-done.30), channel_id=1, source_target_pairs={{0,8},{8,16},{16,24},{24,32},{32,40},{40,48},{48,56},{56,0},{1,9},... | collective-permute-start | bytes 393224 | tf_op jit(solution)/shard_map/ppermute | solution.py:23
  143.2 10.0 %collective-permute-done.28 = bf16[2,256,128]{2,1,0:T(8,128)(2,1)S(1)} collective-permute-done((bf16[2,256,128]{2,1,0:T(8,128)(2,1)S(1)}, bf16[2,256,128]{2,1,0:T(8,128)(2,1)S(1)}, u32[]{:S(2)}, u32[]{:S(2)}) %collective-permute-start.28) | collective-permute-done | bytes 131104 | tf_op jit(solution)/shard_map/ppermute | solution.py:25
  162.1 3.3 %collective-permute-start.44 = (bf16[4,2,256,128]{3,2,1,0:T(8,128)(2,1)S(1)}, bf16[4,2,256,128]{3,2,1,0:T(8,128)(2,1)S(1)}, u32[]{:S(2)}, u32[]{:S(2)}) collective-permute-start(bf16[4,2,256,128]{3,2,1,0:T(8,128)(2,1)S(1)} %collective-permute-done.42), channel_id=1, source_target_pairs={{0,8},{8,16},{16,24},{24,32},{32,40},{40,48},{48,56},{56,0},{1,9},... | collective-permute-start | bytes 1572872 | tf_op jit(solution)/shard_map/ppermute | solution.py:23
  165.8 8.6 %collective-permute-done.44 = bf16[4,2,256,128]{3,2,1,0:T(8,128)(2,1)S(1)} collective-permute-done((bf16[4,2,256,128]{3,2,1,0:T(8,128)(2,1)S(1)}, bf16[4,2,256,128]{3,2,1,0:T(8,128)(2,1)S(1)}, u32[]{:S(2)}, u32[]{:S(2)}) %collective-permute-start.44) | collective-permute-done | bytes 524320 | tf_op jit(solution)/shard_map/ppermute | solution.py:23
  174.4 3.7 %collective-permute-start.46 = (bf16[4,2,256,128]{3,2,1,0:T(8,128)(2,1)S(1)}, bf16[4,2,256,128]{3,2,1,0:T(8,128)(2,1)S(1)}, u32[]{:S(2)}, u32[]{:S(2)}) collective-permute-start(bf16[4,2,256,128]{3,2,1,0:T(8,128)(2,1)S(1)} %collective-permute-done.44), channel_id=1, source_target_pairs={{0,8},{8,16},{16,24},{24,32},{32,40},{40,48},{48,56},{56,0},{1,9},... | collective-permute-start | bytes 1572872 | tf_op jit(solution)/shard_map/ppermute | solution.py:23
  186.9 3.5 %collective-permute-start.48 = (bf16[2,2,256,128]{3,2,1,0:T(8,128)(2,1)}, bf16[2,2,256,128]{3,2,1,0:T(8,128)(2,1)S(1)}, u32[]{:S(2)}, u32[]{:S(2)}) collective-permute-start(bf16[2,2,256,128]{3,2,1,0:T(8,128)(2,1)} %slice.273), channel_id=1, source_target_pairs={{0,8},{8,16},{16,24},{24,32},{32,40},{40,48},{48,56},{56,0},{1,9},... | collective-permute-start | bytes 786440 | tf_op jit(solution)/shard_map/ppermute | solution.py:29
  194.7 5.2 %collective-permute-done.49 = bf16[2,2,256,128]{3,2,1,0:T(8,128)(2,1)} collective-permute-done((bf16[2,2,256,128]{3,2,1,0:T(8,128)(2,1)}, bf16[2,2,256,128]{3,2,1,0:T(8,128)(2,1)}, u32[]{:S(2)}, u32[]{:S(2)}) %collective-permute-start.49) | collective-permute-done | bytes 262176 | tf_op jit(solution)/shard_map/ppermute | solution.py:30
  199.9 4.9 %shard_map.56 = bf16[2,256,128]{2,1,0:T(8,128)(2,1)} custom-call(s32[48]{0:T(128)} %reshape.163.table_ref, bf16[2,8,256,256]{3,2,1,0:T(8,128)(2,1)} %get-tuple-element.69.f_hbm, bf16[2,256,128]{2,1,0:T(8,128)(2,1)} %bitcast.229, bf16[2,256,256]{2,1,0:T(8,128)(2,1)} %get-tuple-element.72.d_hbm, bf16[16,256,128]{2,1,0:T(8,128)(2,1)} %bitcast.170, ...), custom_call_target="tpu_custom_call" | custom-call | tf_op jit(solution)/shard_map/pallas_call | solution.py:103
  216.6 3.7 %collective-permute-start.66 = (bf16[1,256,128]{2,1,0:T(8,128)(2,1)S(1)}, bf16[1,256,128]{2,1,0:T(8,128)(2,1)S(1)}, u32[]{:S(2)}, u32[]{:S(2)}) collective-permute-start(bf16[1,256,128]{2,1,0:T(8,128)(2,1)S(1)} %slice.283), channel_id=1, source_target_pairs={{0,192},{64,0},{128,64},{192,128},{1,193},{65,1},{129,65},{193,129... | collective-permute-start | bytes 196616 | tf_op jit(solution)/shard_map/ppermute | solution.py:30
  228.2 3.4 %collective-permute-start.56 = (bf16[2,256,128]{2,1,0:T(8,128)(2,1)S(1)}, bf16[2,256,128]{2,1,0:T(8,128)(2,1)S(1)}, u32[]{:S(2)}, u32[]{:S(2)}) collective-permute-start(bf16[2,256,128]{2,1,0:T(8,128)(2,1)S(1)} %collective-permute-done.55), channel_id=1, source_target_pairs={{0,8},{8,16},{16,24},{24,32},{32,40},{40,48},{48,56},{56,0},{1,9},... | collective-permute-start | bytes 393224 | tf_op jit(solution)/shard_map/ppermute | solution.py:23
  231.7 9.5 %collective-permute-done.53 = bf16[2,256,128]{2,1,0:T(8,128)(2,1)S(1)} collective-permute-done((bf16[2,256,128]{2,1,0:T(8,128)(2,1)S(1)}, bf16[2,256,128]{2,1,0:T(8,128)(2,1)S(1)}, u32[]{:S(2)}, u32[]{:S(2)}) %collective-permute-start.53) | collective-permute-done | bytes 131104 | tf_op jit(solution)/shard_map/ppermute | solution.py:25
  250.0 3.3 %collective-permute-start.69 = (bf16[4,2,256,128]{3,2,1,0:T(8,128)(2,1)S(1)}, bf16[4,2,256,128]{3,2,1,0:T(8,128)(2,1)S(1)}, u32[]{:S(2)}, u32[]{:S(2)}) collective-permute-start(bf16[4,2,256,128]{3,2,1,0:T(8,128)(2,1)S(1)} %collective-permute-done.67), channel_id=1, source_target_pairs={{0,8},{8,16},{16,24},{24,32},{32,40},{40,48},{48,56},{56,0},{1,9},... | collective-permute-start | bytes 1572872 | tf_op jit(solution)/shard_map/ppermute | solution.py:23
  253.4 8.4 %collective-permute-done.69 = bf16[4,2,256,128]{3,2,1,0:T(8,128)(2,1)S(1)} collective-permute-done((bf16[4,2,256,128]{3,2,1,0:T(8,128)(2,1)S(1)}, bf16[4,2,256,128]{3,2,1,0:T(8,128)(2,1)S(1)}, u32[]{:S(2)}, u32[]{:S(2)}) %collective-permute-start.69) | collective-permute-done | bytes 524320 | tf_op jit(solution)/shard_map/ppermute | solution.py:23
  261.8 3.6 %collective-permute-start.71 = (bf16[4,2,256,128]{3,2,1,0:T(8,128)(2,1)S(1)}, bf16[4,2,256,128]{3,2,1,0:T(8,128)(2,1)S(1)}, u32[]{:S(2)}, u32[]{:S(2)}) collective-permute-start(bf16[4,2,256,128]{3,2,1,0:T(8,128)(2,1)S(1)} %collective-permute-done.69), channel_id=1, source_target_pairs={{0,8},{8,16},{16,24},{24,32},{32,40},{40,48},{48,56},{56,0},{1,9},... | collective-permute-start | bytes 1572872 | tf_op jit(solution)/shard_map/ppermute | solution.py:23
  265.6 3.5 %collective-permute-done.59 = bf16[8,2,256,128]{3,2,1,0:T(8,128)(2,1)S(1)} collective-permute-done((bf16[8,2,256,128]{3,2,1,0:T(8,128)(2,1)S(1)}, bf16[8,2,256,128]{3,2,1,0:T(8,128)(2,1)S(1)}, u32[]{:S(2)}, u32[]{:S(2)}) %collective-permute-start.59) | collective-permute-done | bytes 1048608 | tf_op jit(solution)/shard_map/ppermute | solution.py:23
  271.0 3.4 %collective-permute-start.62 = (bf16[4,2,256,128]{3,2,1,0:T(8,128)(2,1)}, bf16[4,2,256,128]{3,2,1,0:T(8,128)(2,1)}, u32[]{:S(2)}, u32[]{:S(2)}) collective-permute-start(bf16[4,2,256,128]{3,2,1,0:T(8,128)(2,1)} %slice.280), channel_id=1, source_target_pairs={{0,192},{64,0},{128,64},{192,128},{1,193},{65,1},{129,65},{193,129... | collective-permute-start | bytes 1572872 | tf_op jit(solution)/shard_map/ppermute | solution.py:30
  283.5 5.2 %collective-permute-done.74 = bf16[2,2,256,128]{3,2,1,0:T(8,128)(2,1)} collective-permute-done((bf16[2,2,256,128]{3,2,1,0:T(8,128)(2,1)}, bf16[2,2,256,128]{3,2,1,0:T(8,128)(2,1)}, u32[]{:S(2)}, u32[]{:S(2)}) %collective-permute-start.74) | collective-permute-done | bytes 262176 | tf_op jit(solution)/shard_map/ppermute | solution.py:30
  288.8 5.8 %shard_map.57 = bf16[2,256,128]{2,1,0:T(8,128)(2,1)} custom-call(s32[48]{0:T(128)} %reshape.178.table_ref, bf16[2,8,256,256]{3,2,1,0:T(8,128)(2,1)} %get-tuple-element.71.f_hbm, bf16[2,256,128]{2,1,0:T(8,128)(2,1)} %bitcast.228, bf16[2,256,256]{2,1,0:T(8,128)(2,1)} %get-tuple-element.74.d_hbm, bf16[16,256,128]{2,1,0:T(8,128)(2,1)} %bitcast.171, ...), custom_call_target="tpu_custom_call" | custom-call | tf_op jit(solution)/shard_map/pallas_call | solution.py:103
  (323 shorter events, 126.4 us)
Async XLA Ops:
  1.9 13.8 %all-to-all-start = ((bf16[512,4,128]{2,0,1:T(8,128)(2,1)}), bf16[512,4,128]{2,0,1:T(8,128)(2,1)S(1)}, u32[]{:S(2)}, u32[]{:S(2)}) async-start(bf16[512,4,128]{2,0,1:T(8,128)(2,1)} %copy_bitcast_fusion), calls=%async_computation | async-start | bytes 1048576 | tf_op jit(solution)/shard_map/all_to_all | solution.py:123
  36.7 25.8 %collective-permute-start.17 = (bf16[4,2,256,128]{3,2,1,0:T(8,128)(2,1)S(1)}, bf16[4,2,256,128]{3,2,1,0:T(8,128)(2,1)S(1)}, u32[]{:S(2)}, u32[]{:S(2)}) collective-permute-start(bf16[4,2,256,128]{3,2,1,0:T(8,128)(2,1)S(1)} %pad_maximum_fusion), channel_id=1, source_target_pairs={{0,8},{8,16},{16,24},{24,32},{32,40},{40,48},{48,56},{56,0},{1,9},... | collective-permute-start | bytes 1572872 | tf_op jit(solution)/shard_map/ppermute | solution.py:23
  38.6 27.4 %collective-permute-start.18 = (bf16[4,2,256,128]{3,2,1,0:T(8,128)(2,1)S(1)}, bf16[4,2,256,128]{3,2,1,0:T(8,128)(2,1)S(1)}, u32[]{:S(2)}, u32[]{:S(2)}) collective-permute-start(bf16[4,2,256,128]{3,2,1,0:T(8,128)(2,1)S(1)} %pad_maximum_fusion), channel_id=1, source_target_pairs={{0,56},{8,0},{16,8},{24,16},{32,24},{40,32},{48,40},{56,48},{1,57}... | collective-permute-start | bytes 1572872 | tf_op jit(solution)/shard_map/ppermute | solution.py:25
  38.8 14.7 %collective-permute-start.3 = (bf16[2,256,128]{2,1,0:T(8,128)(2,1)S(1)}, bf16[2,256,128]{2,1,0:T(8,128)(2,1)S(1)}, u32[]{:S(2)}, u32[]{:S(2)}) collective-permute-start(bf16[2,256,128]{2,1,0:T(8,128)(2,1)S(1)} %collective-permute-done.2), channel_id=1, source_target_pairs={{0,56},{8,0},{16,8},{24,16},{32,24},{40,32},{48,40},{56,48},{1,57}... | collective-permute-start | bytes 393224 | tf_op jit(solution)/shard_map/ppermute | solution.py:25
  38.9 14.7 %collective-permute-start.6 = (bf16[2,256,128]{2,1,0:T(8,128)(2,1)S(1)}, bf16[2,256,128]{2,1,0:T(8,128)(2,1)S(1)}, u32[]{:S(2)}, u32[]{:S(2)}) collective-permute-start(bf16[2,256,128]{2,1,0:T(8,128)(2,1)S(1)} %collective-permute-done.5), channel_id=1, source_target_pairs={{0,8},{8,16},{16,24},{24,32},{32,40},{40,48},{48,56},{56,0},{1,9},... | collective-permute-start | bytes 393224 | tf_op jit(solution)/shard_map/ppermute | solution.py:23
  59.1 22.3 %collective-permute-start.9 = (bf16[8,2,256,128]{3,2,1,0:T(8,128)(2,1)S(1)}, bf16[8,2,256,128]{3,2,1,0:T(8,128)(2,1)S(1)}, u32[]{:S(2)}, u32[]{:S(2)}) collective-permute-start(bf16[8,2,256,128]{3,2,1,0:T(8,128)(2,1)S(1)} %bitcast_dynamic-update-slice_fusion.14), channel_id=1, source_target_pairs={{0,64},{64,128},{128,192},{192,0},{1,65},{65,129},{129,193},{193,1... | collective-permute-start | bytes 3145736 | tf_op jit(solution)/shard_map/ppermute | solution.py:23
  59.2 23.1 %collective-permute-start.10 = (bf16[8,2,256,128]{3,2,1,0:T(8,128)(2,1)S(1)}, bf16[8,2,256,128]{3,2,1,0:T(8,128)(2,1)S(1)}, u32[]{:S(2)}, u32[]{:S(2)}) collective-permute-start(bf16[8,2,256,128]{3,2,1,0:T(8,128)(2,1)S(1)} %bitcast_dynamic-update-slice_fusion.14), channel_id=1, source_target_pairs={{0,192},{64,0},{128,64},{192,128},{1,193},{65,1},{129,65},{193,129... | collective-permute-start | bytes 3145736 | tf_op jit(solution)/shard_map/ppermute | solution.py:25
  62.5 13.6 %collective-permute-start.19 = (bf16[4,2,256,128]{3,2,1,0:T(8,128)(2,1)S(1)}, bf16[4,2,256,128]{3,2,1,0:T(8,128)(2,1)S(1)}, u32[]{:S(2)}, u32[]{:S(2)}) collective-permute-start(bf16[4,2,256,128]{3,2,1,0:T(8,128)(2,1)S(1)} %collective-permute-done.17), channel_id=1, source_target_pairs={{0,8},{8,16},{16,24},{24,32},{32,40},{40,48},{48,56},{56,0},{1,9},... | collective-permute-start | bytes 1572872 | tf_op jit(solution)/shard_map/ppermute | solution.py:23
  66.0 14.0 %collective-permute-start.20 = (bf16[4,2,256,128]{3,2,1,0:T(8,128)(2,1)S(1)}, bf16[4,2,256,128]{3,2,1,0:T(8,128)(2,1)S(1)}, u32[]{:S(2)}, u32[]{:S(2)}) collective-permute-start(bf16[4,2,256,128]{3,2,1,0:T(8,128)(2,1)S(1)} %collective-permute-done.18), channel_id=1, source_target_pairs={{0,56},{8,0},{16,8},{24,16},{32,24},{40,32},{48,40},{56,48},{1,57}... | collective-permute-start | bytes 1572872 | tf_op jit(solution)/shard_map/ppermute | solution.py:25
  76.1 13.2 %collective-permute-start.21 = (bf16[4,2,256,128]{3,2,1,0:T(8,128)(2,1)S(1)}, bf16[4,2,256,128]{3,2,1,0:T(8,128)(2,1)S(1)}, u32[]{:S(2)}, u32[]{:S(2)}) collective-permute-start(bf16[4,2,256,128]{3,2,1,0:T(8,128)(2,1)S(1)} %collective-permute-done.19), channel_id=1, source_target_pairs={{0,8},{8,16},{16,24},{24,32},{32,40},{40,48},{48,56},{56,0},{1,9},... | collective-permute-start | bytes 1572872 | tf_op jit(solution)/shard_map/ppermute | solution.py:23
  80.0 13.7 %collective-permute-start.22 = (bf16[4,2,256,128]{3,2,1,0:T(8,128)(2,1)S(1)}, bf16[4,2,256,128]{3,2,1,0:T(8,128)(2,1)S(1)}, u32[]{:S(2)}, u32[]{:S(2)}) collective-permute-start(bf16[4,2,256,128]{3,2,1,0:T(8,128)(2,1)S(1)} %collective-permute-done.20), channel_id=1, source_target_pairs={{0,56},{8,0},{16,8},{24,16},{32,24},{40,32},{48,40},{56,48},{1,57}... | collective-permute-start | bytes 1572872 | tf_op jit(solution)/shard_map/ppermute | solution.py:25
  82.3 20.8 %collective-permute-start.11 = (bf16[4,2,256,128]{3,2,1,0:T(8,128)(2,1)}, bf16[4,2,256,128]{3,2,1,0:T(8,128)(2,1)}, u32[]{:S(2)}, u32[]{:S(2)}) collective-permute-start(bf16[4,2,256,128]{3,2,1,0:T(8,128)(2,1)} %slice.257), channel_id=1, source_target_pairs={{0,64},{64,128},{128,192},{192,0},{1,65},{65,129},{129,193},{193,1... | collective-permute-start | bytes 1572872 | tf_op jit(solution)/shard_map/ppermute | solution.py:29
  83.3 19.9 %collective-permute-start.12 = (bf16[4,2,256,128]{3,2,1,0:T(8,128)(2,1)}, bf16[4,2,256,128]{3,2,1,0:T(8,128)(2,1)}, u32[]{:S(2)}, u32[]{:S(2)}) collective-permute-start(bf16[4,2,256,128]{3,2,1,0:T(8,128)(2,1)} %slice.258), channel_id=1, source_target_pairs={{0,192},{64,0},{128,64},{192,128},{1,193},{65,1},{129,65},{193,129... | collective-permute-start | bytes 1572872 | tf_op jit(solution)/shard_map/ppermute | solution.py:30
  110.6 21.5 %collective-permute-start.26 = (bf16[2,256,128]{2,1,0:T(8,128)(2,1)S(1)}, bf16[2,256,128]{2,1,0:T(8,128)(2,1)S(1)}, u32[]{:S(2)}, u32[]{:S(2)}) collective-permute-start(bf16[2,256,128]{2,1,0:T(8,128)(2,1)S(1)} %get-tuple-element.83), channel_id=1, source_target_pairs={{0,56},{8,0},{16,8},{24,16},{32,24},{40,32},{48,40},{56,48},{1,57}... | collective-permute-start | bytes 393224 | tf_op jit(solution)/shard_map/ppermute | solution.py:25
  110.7 21.5 %collective-permute-start.29 = (bf16[2,256,128]{2,1,0:T(8,128)(2,1)S(1)}, bf16[2,256,128]{2,1,0:T(8,128)(2,1)S(1)}, u32[]{:S(2)}, u32[]{:S(2)}) collective-permute-start(bf16[2,256,128]{2,1,0:T(8,128)(2,1)S(1)} %get-tuple-element.83), channel_id=1, source_target_pairs={{0,8},{8,16},{16,24},{24,32},{32,40},{40,48},{48,56},{56,0},{1,9},... | collective-permute-start | bytes 393224 | tf_op jit(solution)/shard_map/ppermute | solution.py:23
  137.7 24.4 %collective-permute-start.42 = (bf16[4,2,256,128]{3,2,1,0:T(8,128)(2,1)S(1)}, bf16[4,2,256,128]{3,2,1,0:T(8,128)(2,1)S(1)}, u32[]{:S(2)}, u32[]{:S(2)}) collective-permute-start(bf16[4,2,256,128]{3,2,1,0:T(8,128)(2,1)S(1)} %pad_maximum_fusion.1), channel_id=1, source_target_pairs={{0,8},{8,16},{16,24},{24,32},{32,40},{40,48},{48,56},{56,0},{1,9},... | collective-permute-start | bytes 1572872 | tf_op jit(solution)/shard_map/ppermute | solution.py:23
  138.3 27.1 %collective-permute-start.43 = (bf16[4,2,256,128]{3,2,1,0:T(8,128)(2,1)S(1)}, bf16[4,2,256,128]{3,2,1,0:T(8,128)(2,1)S(1)}, u32[]{:S(2)}, u32[]{:S(2)}) collective-permute-start(bf16[4,2,256,128]{3,2,1,0:T(8,128)(2,1)S(1)} %pad_maximum_fusion.1), channel_id=1, source_target_pairs={{0,56},{8,0},{16,8},{24,16},{32,24},{40,32},{48,40},{56,48},{1,57}... | collective-permute-start | bytes 1572872 | tf_op jit(solution)/shard_map/ppermute | solution.py:25
  139.8 13.4 %collective-permute-start.28 = (bf16[2,256,128]{2,1,0:T(8,128)(2,1)S(1)}, bf16[2,256,128]{2,1,0:T(8,128)(2,1)S(1)}, u32[]{:S(2)}, u32[]{:S(2)}) collective-permute-start(bf16[2,256,128]{2,1,0:T(8,128)(2,1)S(1)} %collective-permute-done.27), channel_id=1, source_target_pairs={{0,56},{8,0},{16,8},{24,16},{32,24},{40,32},{48,40},{56,48},{1,57}... | collective-permute-start | bytes 393224 | tf_op jit(solution)/shard_map/ppermute | solution.py:25
  139.8 13.8 %collective-permute-start.31 = (bf16[2,256,128]{2,1,0:T(8,128)(2,1)S(1)}, bf16[2,256,128]{2,1,0:T(8,128)(2,1)S(1)}, u32[]{:S(2)}, u32[]{:S(2)}) collective-permute-start(bf16[2,256,128]{2,1,0:T(8,128)(2,1)S(1)} %collective-permute-done.30), channel_id=1, source_target_pairs={{0,8},{8,16},{16,24},{24,32},{32,40},{40,48},{48,56},{56,0},{1,9},... | collective-permute-start | bytes 393224 | tf_op jit(solution)/shard_map/ppermute | solution.py:23
  158.8 22.3 %collective-permute-start.34 = (bf16[8,2,256,128]{3,2,1,0:T(8,128)(2,1)S(1)}, bf16[8,2,256,128]{3,2,1,0:T(8,128)(2,1)S(1)}, u32[]{:S(2)}, u32[]{:S(2)}) collective-permute-start(bf16[8,2,256,128]{3,2,1,0:T(8,128)(2,1)S(1)} %bitcast_dynamic-update-slice_fusion.7), channel_id=1, source_target_pairs={{0,64},{64,128},{128,192},{192,0},{1,65},{65,129},{129,193},{193,1... | collective-permute-start | bytes 3145736 | tf_op jit(solution)/shard_map/ppermute | solution.py:23
  158.9 23.1 %collective-permute-start.35 = (bf16[8,2,256,128]{3,2,1,0:T(8,128)(2,1)S(1)}, bf16[8,2,256,128]{3,2,1,0:T(8,128)(2,1)S(1)}, u32[]{:S(2)}, u32[]{:S(2)}) collective-permute-start(bf16[8,2,256,128]{3,2,1,0:T(8,128)(2,1)S(1)} %bitcast_dynamic-update-slice_fusion.7), channel_id=1, source_target_pairs={{0,192},{64,0},{128,64},{192,128},{1,193},{65,1},{129,65},{193,129... | collective-permute-start | bytes 3145736 | tf_op jit(solution)/shard_map/ppermute | solution.py:25
  165.4 13.3 %collective-permute-start.45 = (bf16[4,2,256,128]{3,2,1,0:T(8,128)(2,1)S(1)}, bf16[4,2,256,128]{3,2,1,0:T(8,128)(2,1)S(1)}, u32[]{:S(2)}, u32[]{:S(2)}) collective-permute-start(bf16[4,2,256,128]{3,2,1,0:T(8,128)(2,1)S(1)} %collective-permute-done.43), channel_id=1, source_target_pairs={{0,56},{8,0},{16,8},{24,16},{32,24},{40,32},{48,40},{56,48},{1,57}... | collective-permute-start | bytes 1572872 | tf_op jit(solution)/shard_map/ppermute | solution.py:25
  226.1 24.0 %collective-permute-start.67 = (bf16[4,2,256,128]{3,2,1,0:T(8,128)(2,1)S(1)}, bf16[4,2,256,128]{3,2,1,0:T(8,128)(2,1)S(1)}, u32[]{:S(2)}, u32[]{:S(2)}) collective-permute-start(bf16[4,2,256,128]{3,2,1,0:T(8,128)(2,1)S(1)} %pad_maximum_fusion.2), channel_id=1, source_target_pairs={{0,8},{8,16},{16,24},{24,32},{32,40},{40,48},{48,56},{56,0},{1,9},... | collective-permute-start | bytes 1572872 | tf_op jit(solution)/shard_map/ppermute | solution.py:23
  226.2 27.2 %collective-permute-start.68 = (bf16[4,2,256,128]{3,2,1,0:T(8,128)(2,1)S(1)}, bf16[4,2,256,128]{3,2,1,0:T(8,128)(2,1)S(1)}, u32[]{:S(2)}, u32[]{:S(2)}) collective-permute-start(bf16[4,2,256,128]{3,2,1,0:T(8,128)(2,1)S(1)} %pad_maximum_fusion.2), channel_id=1, source_target_pairs={{0,56},{8,0},{16,8},{24,16},{32,24},{40,32},{48,40},{56,48},{1,57}... | collective-permute-start | bytes 1572872 | tf_op jit(solution)/shard_map/ppermute | solution.py:25
  228.2 13.0 %collective-permute-start.53 = (bf16[2,256,128]{2,1,0:T(8,128)(2,1)S(1)}, bf16[2,256,128]{2,1,0:T(8,128)(2,1)S(1)}, u32[]{:S(2)}, u32[]{:S(2)}) collective-permute-start(bf16[2,256,128]{2,1,0:T(8,128)(2,1)S(1)} %collective-permute-done.52), channel_id=1, source_target_pairs={{0,56},{8,0},{16,8},{24,16},{32,24},{40,32},{48,40},{56,48},{1,57}... | collective-permute-start | bytes 393224 | tf_op jit(solution)/shard_map/ppermute | solution.py:25
  228.2 13.8 %collective-permute-start.56 = (bf16[2,256,128]{2,1,0:T(8,128)(2,1)S(1)}, bf16[2,256,128]{2,1,0:T(8,128)(2,1)S(1)}, u32[]{:S(2)}, u32[]{:S(2)}) collective-permute-start(bf16[2,256,128]{2,1,0:T(8,128)(2,1)S(1)} %collective-permute-done.55), channel_id=1, source_target_pairs={{0,8},{8,16},{16,24},{24,32},{32,40},{40,48},{48,56},{56,0},{1,9},... | collective-permute-start | bytes 393224 | tf_op jit(solution)/shard_map/ppermute | solution.py:23
  246.7 22.4 %collective-permute-start.59 = (bf16[8,2,256,128]{3,2,1,0:T(8,128)(2,1)S(1)}, bf16[8,2,256,128]{3,2,1,0:T(8,128)(2,1)S(1)}, u32[]{:S(2)}, u32[]{:S(2)}) collective-permute-start(bf16[8,2,256,128]{3,2,1,0:T(8,128)(2,1)S(1)} %bitcast_dynamic-update-slice_fusion), channel_id=1, source_target_pairs={{0,64},{64,128},{128,192},{192,0},{1,65},{65,129},{129,193},{193,1... | collective-permute-start | bytes 3145736 | tf_op jit(solution)/shard_map/ppermute | solution.py:23
  246.8 23.3 %collective-permute-start.60 = (bf16[8,2,256,128]{3,2,1,0:T(8,128)(2,1)S(1)}, bf16[8,2,256,128]{3,2,1,0:T(8,128)(2,1)S(1)}, u32[]{:S(2)}, u32[]{:S(2)}) collective-permute-start(bf16[8,2,256,128]{3,2,1,0:T(8,128)(2,1)S(1)} %bitcast_dynamic-update-slice_fusion), channel_id=1, source_target_pairs={{0,192},{64,0},{128,64},{192,128},{1,193},{65,1},{129,65},{193,129... | collective-permute-start | bytes 3145736 | tf_op jit(solution)/shard_map/ppermute | solution.py:25
  261.8 13.5 %collective-permute-start.71 = (bf16[4,2,256,128]{3,2,1,0:T(8,128)(2,1)S(1)}, bf16[4,2,256,128]{3,2,1,0:T(8,128)(2,1)S(1)}, u32[]{:S(2)}, u32[]{:S(2)}) collective-permute-start(bf16[4,2,256,128]{3,2,1,0:T(8,128)(2,1)S(1)} %collective-permute-done.69), channel_id=1, source_target_pairs={{0,8},{8,16},{16,24},{24,32},{32,40},{40,48},{48,56},{56,0},{1,9},... | collective-permute-start | bytes 1572872 | tf_op jit(solution)/shard_map/ppermute | solution.py:23
  265.6 13.7 %collective-permute-start.72 = (bf16[4,2,256,128]{3,2,1,0:T(8,128)(2,1)S(1)}, bf16[4,2,256,128]{3,2,1,0:T(8,128)(2,1)S(1)}, u32[]{:S(2)}, u32[]{:S(2)}) collective-permute-start(bf16[4,2,256,128]{3,2,1,0:T(8,128)(2,1)S(1)} %collective-permute-done.70), channel_id=1, source_target_pairs={{0,56},{8,0},{16,8},{24,16},{32,24},{40,32},{48,40},{56,48},{1,57}... | collective-permute-start | bytes 1572872 | tf_op jit(solution)/shard_map/ppermute | solution.py:25
  270.1 18.6 %collective-permute-start.61 = (bf16[4,2,256,128]{3,2,1,0:T(8,128)(2,1)}, bf16[4,2,256,128]{3,2,1,0:T(8,128)(2,1)}, u32[]{:S(2)}, u32[]{:S(2)}) collective-permute-start(bf16[4,2,256,128]{3,2,1,0:T(8,128)(2,1)} %slice.279), channel_id=1, source_target_pairs={{0,64},{64,128},{128,192},{192,0},{1,65},{65,129},{129,193},{193,1... | collective-permute-start | bytes 1572872 | tf_op jit(solution)/shard_map/ppermute | solution.py:29
  271.0 17.7 %collective-permute-start.62 = (bf16[4,2,256,128]{3,2,1,0:T(8,128)(2,1)}, bf16[4,2,256,128]{3,2,1,0:T(8,128)(2,1)}, u32[]{:S(2)}, u32[]{:S(2)}) collective-permute-start(bf16[4,2,256,128]{3,2,1,0:T(8,128)(2,1)} %slice.280), channel_id=1, source_target_pairs={{0,192},{64,0},{128,64},{192,128},{1,193},{65,1},{129,65},{193,129... | collective-permute-start | bytes 1572872 | tf_op jit(solution)/shard_map/ppermute | solution.py:30
  (103 other events, 1819.2 us)

commit v5 on v3

--- a/solution.py
+++ b/solution.py
@@ -8,15 +8,24 @@
 LEV = 4
 
 
-def level_solve(table, factor, right, dinv, sources, slot_count):
+def level_solve(table, factor, right, dinv, sources, slot_count, earlier=()):
     per_level, _, block, _ = factor.shape
     width = right.shape[-1]
     n_src = len(sources)
+    n_early = len(earlier)
     total = per_level * slot_count
 
     def kernel(table_ref, f_hbm, r_hbm, d_hbm, *rest):
         src = rest[:n_src]
-        o_ref, xs, fs, rs, ds, acc, sem, fsem, rsem = rest[n_src:]
+        early = rest[n_src : n_src + n_early]
+        o_ref, xs, fs, rs, ds, acc, sem, fsem, rsem, esem = rest[n_src + n_early :]
+        done = per_level * n_early
+        ecopies = [
+            pltpu.make_async_copy(e, o_ref.at[pl.ds(i * per_level, per_level)], esem.at[i])
+            for i, e in enumerate(early)
+        ]
+        for c in ecopies:
+            c.start()
         rcopy = pltpu.make_async_copy(r_hbm, rs, rsem.at[0])
         dcopy = pltpu.make_async_copy(d_hbm, ds, rsem.at[1])
         slots = []
@@ -40,6 +49,8 @@
         dcopy.start()
         rcopy.wait()
         dcopy.wait()
+        for c in ecopies:
+            c.wait()
         for b in range(per_level):
             acc[...] = jnp.zeros_like(acc)
             for k in range(slot_count):
@@ -53,12 +64,13 @@
                     acc[...] += jnp.dot(fs[s], xs[s], preferred_element_type=jnp.float32)
 
             residual = (rs[b].astype(jnp.float32) - acc[...]).astype(jnp.bfloat16)
-            o_ref[b] = jnp.dot(ds[b], residual, preferred_element_type=jnp.float32).astype(o_ref.dtype)
+            o_ref[done + b] = jnp.dot(ds[b], residual, preferred_element_type=jnp.float32).astype(o_ref.dtype)
 
     any_spec = pl.BlockSpec(memory_space=pl.ANY)
     return pl.pallas_call(
         kernel,
-        in_specs=[pl.BlockSpec(memory_space=pltpu.SMEM), any_spec, any_spec, any_spec] + [any_spec] * n_src,
+        in_specs=[pl.BlockSpec(memory_space=pltpu.SMEM), any_spec, any_spec, any_spec]
+        + [any_spec] * (n_src + n_early),
         out_specs=pl.BlockSpec(memory_space=pltpu.VMEM),
         scratch_shapes=[
             pltpu.VMEM((total, block, width), sources[0].dtype),
@@ -69,9 +81,10 @@
             pltpu.SemaphoreType.DMA((total,)),
             pltpu.SemaphoreType.DMA((total,)),
             pltpu.SemaphoreType.DMA((2,)),
+            pltpu.SemaphoreType.DMA((max(n_early, 1),)),
         ],
-        out_shape=jax.ShapeDtypeStruct((per_level, block, width), jnp.bfloat16),
-    )(table, factor, right, dinv, *sources)
+        out_shape=jax.ShapeDtypeStruct((per_level * (n_early + 1), block, width), jnp.bfloat16),
+    )(table, factor, right, dinv, *sources, *earlier)
 
 
 def shards(kernel_rows, factor_blocks, diag_inverse, pattern, live_counts):
@@ -109,11 +122,12 @@
                 diag_inverse[lower:upper],
                 gathered_all,
                 slot_count,
+                earlier=tuple(solved_all) if level_now + 1 == LEV else (),
             )
-        solved_all.append(solved)
         if level_now + 1 < LEV:
+            solved_all.append(solved)
             gathered_all.append(lax.all_gather(solved, "rows", axis=0, tiled=True))
-    return jnp.concatenate(solved_all, axis=0).reshape(per_device * block, width)
+    return solved.reshape(per_device * block, width)
 
 
 def solution(mesh):

time: 296 us -> 294 us (level)
  no operation moved by 1% of the time
where the time goes in v5:
time: 294 us; the launch traced here: 292 us
  waiting for transfers between devices  238 us (81%)
  Pallas kernels  16.3 us (6%)
  between operations  13.2 us (4%)
  blocking collectives  12.6 us (4%)
  local copies, waits for them, and re-layouts  10.4 us (4%)
    all_gather x3, waiting for transfers between devices, shards(): gathered_all.append(lax.all_gather(solved, 'rows', axis=0, tiled=True))  238 us
    pallas_call x3, Pallas kernels, level_solve(): pl.pallas_call(kernel, in_specs=[pl.BlockSpec(memory_space=pltpu.SMEM), a...  16.3 us
    all_to_all x1, blocking collectives, shards(): lax.all_to_all(kernel_rows, 'rhs', split_axis=1, concat_axis=0, tiled=True)  12.6 us
  transfers between devices with their start and end apart: 3, of which 3 were waited for; matrix products, arithmetic and copies ran while one was open for 3% of the time, Pallas kernels for 0%

profile of v5, /device:TPU:2, one launch (start us, length us, event | category | flops | bytes accessed | tf_op | source)
XLA Modules:
  0.0 291.8 jit_solution(6045729902367857911)
XLA Ops:
  6.5 0.0 copy-start
  6.5 0.0 copy-start.1
  6.5 0.0 copy-start.3
  6.5 0.0 copy-start.2
  6.5 0.0 all-gather.4.cloned.1.call-start
  6.6 1.0 copy-done
  7.6 0.1 copy_bitcast_fusion
  7.7 12.6 %all_to_all.16 = bf16[512,4,128]{2,0,1:T(8,128)(2,1)S(1)} all-to-all(bf16[512,4,128]{2,0,1:T(8,128)(2,1)S(1)} %copy_bitcast_fusion), channel_id=1, replica_groups=mesh['rows'=64,'rhs'=4] {'rhs'}, dimensions={1} | all-to-all | bytes 1048576 | tf_op jit(solution)/shard_map/all_to_all | solution.py:91
  20.3 0.8 fusion.13
  21.1 0.0 copy-done.1
  21.1 0.9 convolution_convert_fusion.rest_3_
  22.0 0.0 all-gather.4.cloned.1.call-update
  22.0 0.0 all-gather.6.cloned.1.call-start
  22.1 0.0 copy-done.3
  22.1 0.1 iota_compare_fusion
  22.2 0.0 copy-done.2
  22.2 0.6 reshape.23.table_ref
  22.8 0.9 fusion.12
  23.7 5.7 %fusion.11 = (bf16[2,8,256,256]{3,2,1,0:T(8,128)(2,1)}, bf16[2,8,256,256]{3,2,1,0:T(8,128)(2,1)}, bf16[2,8,256,256]{3,2,1,0:T(8,128)(2,1)}) fusion(bf16[8,8,256,256]{3,2,1,0:T(8,128)(2,1)} %param.6), kind=kLoop, calls=%fused_computation.39 | loop fusion | bytes 12582912 | tf_op jit(solution)/shard_map/slice | solution.py:120
  29.4 77.8 %all-gather.4.cloned.1.call-done.rest_0_ = bf16[128,256,128]{2,1,0:T(8,128)(2,1)} async-done(((bf16[2,256,128]{2,1,0:T(8,128)(2,1)}), bf16[128,256,128]{2,1,0:T(8,128)(2,1)}) %all-gather.4.cloned.1.call-update) | async-done | bytes 8388624 | tf_op jit(solution)/shard_map/all_gather | solution.py:129
  107.2 6.8 %shard_map.55.rest_4_ = bf16[2,256,128]{2,1,0:T(8,128)(2,1)} custom-call(s32[48]{0:T(128)} %reshape.23.table_ref, bf16[2,8,256,256]{3,2,1,0:T(8,128)(2,1)} %get-tuple-element.7.f_hbm, bf16[2,256,128]{2,1,0:T(8,128)(2,1)} %bitcast.34, bf16[2,256,256]{2,1,0:T(8,128)(2,1)} %get-tuple-element.10.d_hbm, bf16[128,256,128]{2,1,0:T(8,128)(2,1)} %all-gather.4.cloned.1.call-done.rest_0_), custom_call_target="tpu_custom_call" | custom-call | tf_op jit(solution)/shard_map/pallas_call | solution.py:70
  114.1 0.0 all-gather.6.cloned.1.call-update
  114.1 0.0 all-gather.8.cloned.1.call-start
  114.2 0.7 reshape.24.table_ref
  114.9 78.8 %all-gather.6.cloned.1.call-done.rest_1_ = bf16[128,256,128]{2,1,0:T(8,128)(2,1)} async-done(((bf16[2,256,128]{2,1,0:T(8,128)(2,1)}), bf16[128,256,128]{2,1,0:T(8,128)(2,1)}) %all-gather.6.cloned.1.call-update) | async-done | bytes 8388624 | tf_op jit(solution)/shard_map/all_gather | solution.py:129
  193.7 3.9 %shard_map.56.rest_5_ = bf16[2,256,128]{2,1,0:T(8,128)(2,1)} custom-call(s32[48]{0:T(128)} %reshape.24.table_ref, bf16[2,8,256,256]{3,2,1,0:T(8,128)(2,1)} %get-tuple-element.5.f_hbm, bf16[2,256,128]{2,1,0:T(8,128)(2,1)} %bitcast.33, bf16[2,256,256]{2,1,0:T(8,128)(2,1)} %get-tuple-element.8.d_hbm, ...), custom_call_target="tpu_custom_call" | custom-call | tf_op jit(solution)/shard_map/pallas_call | solution.py:70
  197.6 0.0 all-gather.8.cloned.1.call-update
  197.6 0.6 reshape.22.table_ref
  198.3 81.4 %all-gather.8.cloned.1.call-done.rest_2_ = bf16[128,256,128]{2,1,0:T(8,128)(2,1)} async-done(((bf16[2,256,128]{2,1,0:T(8,128)(2,1)}), bf16[128,256,128]{2,1,0:T(8,128)(2,1)}) %all-gather.8.cloned.1.call-update) | async-done | bytes 8388624 | tf_op jit(solution)/shard_map/all_gather | solution.py:129
  279.7 5.6 %shard_map.57 = bf16[8,256,128]{2,1,0:T(8,128)(2,1)} custom-call(s32[48]{0:T(128)} %reshape.22.table_ref, bf16[2,8,256,256]{3,2,1,0:T(8,128)(2,1)} %get-tuple-element.6.f_hbm, bf16[2,256,128]{2,1,0:T(8,128)(2,1)} %bitcast.32, bf16[2,256,256]{2,1,0:T(8,128)(2,1)} %get-tuple-element.9.d_hbm, bf16[128,256,128]{2,1,0:T(8,128)(2,1)} %all-gather.4.cloned.1.call-done.rest_0_, ...), custom_call_target="tpu_custom_call" | custom-call | tf_op jit(solution)/shard_map/pallas_call | solution.py:70
  (6 shorter events, 0.1 us)
Async XLA Ops:
  6.5 1.0 copy-start
  6.5 14.6 %copy-start.1 = (bf16[8,256,256]{2,1,0:T(8,128)(2,1)S(1)}, bf16[8,256,256]{2,1,0:T(8,128)(2,1)}, u32[]{:S(2)}) copy-start(bf16[8,256,256]{2,1,0:T(8,128)(2,1)} %param.7) | copy-start | bytes 3145732
  6.5 15.5 %copy-start.3 = (s32[8]{0:T(128)S(1)}, s32[8]{0:T(128)}, u32[]{:S(2)}) copy-start(s32[8]{0:T(128)} %param.9) | copy-start | bytes 100
  6.5 15.6 %copy-start.2 = (s32[8,8]{1,0:T(8,128)S(1)}, s32[8,8]{1,0:T(8,128)}, u32[]{:S(2)}) copy-start(s32[8,8]{1,0:T(8,128)} %param.8) | copy-start | bytes 772
  6.5 100.7 %all-gather.4.cloned.1.call-start = ((), (), s32[]{:S(2)}) async-start(), calls=%async_computation.1 | async-start | bytes 8519680 | tf_op jit(solution)/shard_map/all_gather | solution.py:129
  22.0 171.7 %all-gather.6.cloned.1.call-start = ((), (), s32[]{:S(2)}) async-start(), calls=%async_computation.2 | async-start | bytes 8519680 | tf_op jit(solution)/shard_map/all_gather | solution.py:129
  114.1 165.6 %all-gather.8.cloned.1.call-start = ((), (), s32[]{:S(2)}) async-start(), calls=%async_computation.3 | async-start | bytes 8519680 | tf_op jit(solution)/shard_map/all_gather | solution.py:129
Sparse Core Ops, SparseCore 0:
  22.1 85.0 all-gather.3
  114.2 79.4 all-gather.5
  197.7 81.9 all-gather.7

commit v6 on v5

--- a/solution.py
+++ b/solution.py
@@ -8,17 +8,22 @@
 LEV = 4
 
 
-def level_solve(table, factor, right, dinv, sources, slot_count, earlier=()):
+def level_solve(table, factor, right, dinv, sources, slot_count, earlier=(), init=None):
     per_level, _, block, _ = factor.shape
     width = right.shape[-1]
     n_src = len(sources)
     n_early = len(earlier)
+    n_init = 0 if init is None else 1
     total = per_level * slot_count
 
     def kernel(table_ref, f_hbm, r_hbm, d_hbm, *rest):
         src = rest[:n_src]
         early = rest[n_src : n_src + n_early]
-        o_ref, xs, fs, rs, ds, acc, sem, fsem, rsem, esem = rest[n_src + n_early :]
+        start_ref = rest[n_src + n_early : n_src + n_early + n_init]
+        o_ref, xs, fs, rs, ds, acc, ini, sem, fsem, rsem, esem = rest[n_src + n_early + n_init :]
+        icopies = [pltpu.make_async_copy(r, ini, rsem.at[2]) for r in start_ref]
+        for c in icopies:
+            c.start()
         done = per_level * n_early
         ecopies = [
             pltpu.make_async_copy(e, o_ref.at[pl.ds(i * per_level, per_level)], esem.at[i])
@@ -51,8 +56,13 @@
         dcopy.wait()
         for c in ecopies:
             c.wait()
+        for c in icopies:
+            c.wait()
         for b in range(per_level):
-            acc[...] = jnp.zeros_like(acc)
+            if n_init:
+                acc[...] = ini[b]
+            else:
+                acc[...] = jnp.zeros_like(acc)
             for k in range(slot_count):
                 s = b * slot_count + k
                 used = slots[s][0]
@@ -70,7 +80,7 @@
     return pl.pallas_call(
         kernel,
         in_specs=[pl.BlockSpec(memory_space=pltpu.SMEM), any_spec, any_spec, any_spec]
-        + [any_spec] * (n_src + n_early),
+        + [any_spec] * (n_src + n_early + n_init),
         out_specs=pl.BlockSpec(memory_space=pltpu.VMEM),
         scratch_shapes=[
             pltpu.VMEM((total, block, width), sources[0].dtype),
@@ -78,13 +88,65 @@
             pltpu.VMEM((per_level, block, width), right.dtype),
             pltpu.VMEM((per_level, block, block), dinv.dtype),
             pltpu.VMEM((block, width), jnp.float32),
-            pltpu.SemaphoreType.DMA((total,)),
-            pltpu.SemaphoreType.DMA((total,)),
-            pltpu.SemaphoreType.DMA((2,)),
+            pltpu.VMEM((per_level, block, width), jnp.float32),
+            pltpu.SemaphoreType.DMA((total,)),
+            pltpu.SemaphoreType.DMA((total,)),
+            pltpu.SemaphoreType.DMA((3,)),
             pltpu.SemaphoreType.DMA((max(n_early, 1),)),
         ],
         out_shape=jax.ShapeDtypeStruct((per_level * (n_early + 1), block, width), jnp.bfloat16),
-    )(table, factor, right, dinv, *sources, *earlier)
+    )(table, factor, right, dinv, *sources, *earlier, *([] if init is None else [init]))
+
+
+def partial_sum(table, factor, sources, slot_count, width):
+    per_level, _, block, _ = factor.shape
+    n_src = len(sources)
+    total = per_level * slot_count
+
+    def kernel(table_ref, f_hbm, *rest):
+        src = rest[:n_src]
+        o_ref, xs, fs, sem, fsem = rest[n_src:]
+        slots = []
+        for s in range(total):
+            b, k = divmod(s, slot_count)
+            idx = table_ref[0 * total + s]
+            lv = table_ref[1 * total + s]
+            act = table_ref[2 * total + s]
+            used = (act > 0) & (lv >= 0) & (lv < n_src)
+            slots.append(used)
+            for level in range(n_src):
+                @pl.when((act > 0) & (lv == level))
+                def _():
+                    pltpu.make_async_copy(src[level].at[idx], xs.at[s], sem.at[s]).start()
+
+            @pl.when(used)
+            def _():
+                pltpu.make_async_copy(f_hbm.at[b, k], fs.at[s], fsem.at[s]).start()
+
+        for b in range(per_level):
+            o_ref[b] = jnp.zeros((block, width), jnp.float32)
+            for k in range(slot_count):
+                s = b * slot_count + k
+
+                @pl.when(slots[s])
+                def _():
+                    pltpu.make_async_copy(src[0].at[0], xs.at[s], sem.at[s]).wait()
+                    pltpu.make_async_copy(f_hbm.at[0, 0], fs.at[s], fsem.at[s]).wait()
+                    o_ref[b] += jnp.dot(fs[s], xs[s], preferred_element_type=jnp.float32)
+
+    any_spec = pl.BlockSpec(memory_space=pl.ANY)
+    return pl.pallas_call(
+        kernel,
+        in_specs=[pl.BlockSpec(memory_space=pltpu.SMEM), any_spec] + [any_spec] * n_src,
+        out_specs=pl.BlockSpec(memory_space=pltpu.VMEM),
+        scratch_shapes=[
+            pltpu.VMEM((total, block, width), sources[0].dtype),
+            pltpu.VMEM((total, block, block), factor.dtype),
+            pltpu.SemaphoreType.DMA((total,)),
+            pltpu.SemaphoreType.DMA((total,)),
+        ],
+        out_shape=jax.ShapeDtypeStruct((per_level, block, width), jnp.float32),
+    )(table, factor, *sources)
 
 
 def shards(kernel_rows, factor_blocks, diag_inverse, pattern, live_counts):
@@ -112,17 +174,24 @@
                 preferred_element_type=jnp.float32,
             ).astype(jnp.bfloat16)
         else:
-            table = jnp.stack(
-                [position[lower:upper], level_of[lower:upper], active[lower:upper].astype(jnp.int32)]
-            ).reshape(-1).astype(jnp.int32)
+            newest = level_now - 1
+            pos = position[lower:upper]
+            lv = level_of[lower:upper]
+            act = active[lower:upper].astype(jnp.int32)
+            init = None
+            if newest > 0:
+                old_table = jnp.stack([pos, lv, act]).reshape(-1).astype(jnp.int32)
+                init = partial_sum(old_table, factor_blocks[lower:upper], gathered_all[:newest], slot_count, width)
+            table = jnp.stack([pos, jnp.where(lv == newest, 0, -1), act]).reshape(-1).astype(jnp.int32)
             solved = level_solve(
                 table,
                 factor_blocks[lower:upper],
                 right_side[lower:upper],
                 diag_inverse[lower:upper],
-                gathered_all,
+                gathered_all[newest:],
                 slot_count,
                 earlier=tuple(solved_all) if level_now + 1 == LEV else (),
+                init=init,
             )
         if level_now + 1 < LEV:
             solved_all.append(solved)

time: 294 us -> 292 us (level)
  waiting for transfers between devices: 238 us -> 231 us
  Pallas kernels: 16.3 us -> 21 us
    all_gather x3, waiting for transfers between devices: 238 us -> 231 us  [shards(): gathered_all.append(lax.all_gather(solved, 'rows', axis=0, tiled=True))]
    pallas_call x0 -> x2, Pallas kernels: none -> 6.56 us  [partial_sum(): pl.pallas_call(kernel, in_specs=[pl.BlockSpec(memory_space=pltpu.SMEM), a...]
  transfers between devices with their start and end apart: 3 -> 3, of which waited for: 3 -> 3; matrix products, arithmetic and copies ran while one was open for 3% -> 3% of each run, Pallas kernels for 0% -> 2%
where the time goes in v6:
time: 292 us; the launch traced here: 291 us
  waiting for transfers between devices  231 us (79%)
  Pallas kernels  21 us (7%)
  between operations  13.2 us (5%)
  blocking collectives  12.6 us (4%)
  local copies, waits for them, and re-layouts  11.5 us (4%)
    all_gather x3, waiting for transfers between devices, shards(): gathered_all.append(lax.all_gather(solved, 'rows', axis=0, tiled=True))  231 us
    pallas_call x3, Pallas kernels, level_solve(): pl.pallas_call(kernel, in_specs=[pl.BlockSpec(memory_space=pltpu.SMEM), a...  14.4 us
    all_to_all x1, blocking collectives, shards(): lax.all_to_all(kernel_rows, 'rhs', split_axis=1, concat_axis=0, tiled=True)  12.6 us
    pallas_call x2, Pallas kernels, partial_sum(): pl.pallas_call(kernel, in_specs=[pl.BlockSpec(memory_space=pltpu.SMEM), a...  6.56 us
  transfers between devices with their start and end apart: 3, of which 3 were waited for; matrix products, arithmetic and copies ran while one was open for 3% of the time, Pallas kernels for 2%

profile of v6, /device:TPU:2, one launch (start us, length us, event | category | flops | bytes accessed | tf_op | source)
XLA Modules:
  0.0 290.8 jit_solution(6882292642535560053)
XLA Ops:
  6.5 0.0 copy-start
  6.5 0.0 copy-start.1
  6.5 0.0 all-gather.4.cloned.1.call-start
  6.6 1.0 copy-done
  7.6 0.1 copy_bitcast_fusion
  7.7 12.6 %all_to_all.16 = bf16[512,4,128]{2,0,1:T(8,128)(2,1)S(1)} all-to-all(bf16[512,4,128]{2,0,1:T(8,128)(2,1)S(1)} %copy_bitcast_fusion), channel_id=1, replica_groups=mesh['rows'=64,'rhs'=4] {'rhs'}, dimensions={1} | all-to-all | bytes 1048576 | tf_op jit(solution)/shard_map/all_to_all | solution.py:153
  20.3 0.8 fusion.16
  21.1 0.0 copy-done.1
  21.1 0.9 convolution_convert_fusion.rest_1_
  22.0 0.0 all-gather.4.cloned.1.call-update
  22.0 0.0 all-gather.6.cloned.1.call-start
  22.1 0.0 copy-done.3
  22.1 0.1 iota_compare_fusion
  22.1 0.0 copy-done.2
  22.2 0.6 reshape.30.table_ref
  22.9 0.9 fusion.15
  23.7 5.7 %fusion.14 = (bf16[2,8,256,256]{3,2,1,0:T(8,128)(2,1)}, bf16[2,8,256,256]{3,2,1,0:T(8,128)(2,1)}, bf16[2,8,256,256]{3,2,1,0:T(8,128)(2,1)}) fusion(bf16[8,8,256,256]{3,2,1,0:T(8,128)(2,1)} %param.6), kind=kLoop, calls=%fused_computation.50 | loop fusion | bytes 12582912 | tf_op jit(solution)/shard_map/slice | solution.py:188
  29.4 77.8 %all-gather.4.cloned.1.call-done.rest_0_ = bf16[128,256,128]{2,1,0:T(8,128)(2,1)} async-done(((bf16[2,256,128]{2,1,0:T(8,128)(2,1)}), bf16[128,256,128]{2,1,0:T(8,128)(2,1)}) %all-gather.4.cloned.1.call-update) | async-done | bytes 8388624 | tf_op jit(solution)/shard_map/all_gather | solution.py:198
  107.2 5.5 %shard_map.55.rest_2_ = bf16[2,256,128]{2,1,0:T(8,128)(2,1)} custom-call(s32[48]{0:T(128)} %reshape.30.table_ref, bf16[2,8,256,256]{3,2,1,0:T(8,128)(2,1)} %get-tuple-element.5.f_hbm, bf16[2,256,128]{2,1,0:T(8,128)(2,1)} %bitcast.38, bf16[2,256,256]{2,1,0:T(8,128)(2,1)} %get-tuple-element.8.d_hbm, bf16[128,256,128]{2,1,0:T(8,128)(2,1)} %all-gather.4.cloned.1.call-done.rest_0_), custom_call_target="tpu_custom_call" | custom-call | tf_op jit(solution)/shard_map/pallas_call | solution.py:80
  112.7 0.0 all-gather.6.cloned.1.call-update
  112.8 0.0 all-gather.8.cloned.1.call-start
  112.8 0.6 reshape.29.table_ref
  113.4 0.7 reshape.31.table_ref
  114.1 3.5 %shard_map.56.rest_1_ = f32[2,256,128]{2,1,0:T(8,128)} custom-call(s32[48]{0:T(128)} %reshape.31.table_ref, bf16[2,8,256,256]{3,2,1,0:T(8,128)(2,1)} %get-tuple-element.7.f_hbm, bf16[128,256,128]{2,1,0:T(8,128)(2,1)} %all-gather.4.cloned.1.call-done.rest_0_), custom_call_target="tpu_custom_call" | custom-call | tf_op jit(solution)/shard_map/pallas_call | solution.py:138
  117.6 76.9 %all-gather.6.cloned.1.call-done.rest_0_.rest_1_ = bf16[128,256,128]{2,1,0:T(8,128)(2,1)} async-done(((bf16[2,256,128]{2,1,0:T(8,128)(2,1)}), bf16[128,256,128]{2,1,0:T(8,128)(2,1)}) %all-gather.6.cloned.1.call-update) | async-done | bytes 8388624 | tf_op jit(solution)/shard_map/all_gather | solution.py:198
  194.5 4.6 %shard_map.57.rest_3_ = bf16[2,256,128]{2,1,0:T(8,128)(2,1)} custom-call(s32[48]{0:T(128)} %reshape.29.table_ref, bf16[2,8,256,256]{3,2,1,0:T(8,128)(2,1)} %get-tuple-element.7.f_hbm, bf16[2,256,128]{2,1,0:T(8,128)(2,1)} %bitcast.37, bf16[2,256,256]{2,1,0:T(8,128)(2,1)} %get-tuple-element.9.d_hbm, ...), custom_call_target="tpu_custom_call" | custom-call | tf_op jit(solution)/shard_map/pallas_call | solution.py:80
  199.1 0.0 all-gather.8.cloned.1.call-update
  199.1 0.6 reshape.32.table_ref
  199.7 0.6 reshape.28.table_ref
  200.3 3.1 %shard_map.58.rest_4_ = f32[2,256,128]{2,1,0:T(8,128)} custom-call(s32[48]{0:T(128)} %reshape.32.table_ref, bf16[2,8,256,256]{3,2,1,0:T(8,128)(2,1)} %get-tuple-element.6.f_hbm, bf16[128,256,128]{2,1,0:T(8,128)(2,1)} %all-gather.4.cloned.1.call-done.rest_0_, bf16[128,256,128]{2,1,0:T(8,128)(2,1)} %all-gather.6.cloned.1.call-done.rest_0_.rest_1_), custom_call_target="tpu_custom_call" | custom-call | tf_op jit(solution)/shard_map/pallas_call | solution.py:138
  203.4 76.6 %all-gather.8.cloned.1.call-done.rest_0_ = bf16[128,256,128]{2,1,0:T(8,128)(2,1)} async-done(((bf16[2,256,128]{2,1,0:T(8,128)(2,1)}), bf16[128,256,128]{2,1,0:T(8,128)(2,1)}) %all-gather.8.cloned.1.call-update) | async-done | bytes 8388624 | tf_op jit(solution)/shard_map/all_gather | solution.py:198
  280.0 4.2 %shard_map.59 = bf16[8,256,128]{2,1,0:T(8,128)(2,1)} custom-call(s32[48]{0:T(128)} %reshape.28.table_ref, bf16[2,8,256,256]{3,2,1,0:T(8,128)(2,1)} %get-tuple-element.6.f_hbm, bf16[2,256,128]{2,1,0:T(8,128)(2,1)} %bitcast.36, bf16[2,256,256]{2,1,0:T(8,128)(2,1)} %get-tuple-element.10.d_hbm, bf16[128,256,128]{2,1,0:T(8,128)(2,1)} %all-gather.8.cloned.1.call-done.rest_0_, ...), custom_call_target="tpu_custom_call" | custom-call | tf_op jit(solution)/shard_map/pallas_call | solution.py:80
  (8 shorter events, 0.1 us)
Async XLA Ops:
  6.5 1.0 copy-start
  6.5 14.5 %copy-start.1 = (bf16[8,256,256]{2,1,0:T(8,128)(2,1)S(1)}, bf16[8,256,256]{2,1,0:T(8,128)(2,1)}, u32[]{:S(2)}) copy-start(bf16[8,256,256]{2,1,0:T(8,128)(2,1)} %param.7) | copy-start | bytes 3145732
  6.5 15.5 %copy-start.3 = (s32[8]{0:T(128)S(1)}, s32[8]{0:T(128)}, u32[]{:S(2)}) copy-start(s32[8]{0:T(128)} %param.9) | copy-start | bytes 100
  6.5 15.6 %copy-start.2 = (s32[8,8]{1,0:T(8,128)S(1)}, s32[8,8]{1,0:T(8,128)}, u32[]{:S(2)}) copy-start(s32[8,8]{1,0:T(8,128)} %param.8) | copy-start | bytes 772
  6.5 100.7 %all-gather.4.cloned.1.call-start = ((), (), s32[]{:S(2)}) async-start(), calls=%async_computation.1 | async-start | bytes 8519680 | tf_op jit(solution)/shard_map/all_gather | solution.py:198
  22.0 172.4 %all-gather.6.cloned.1.call-start = ((), (), s32[]{:S(2)}) async-start(), calls=%async_computation.2 | async-start | bytes 8519680 | tf_op jit(solution)/shard_map/all_gather | solution.py:198
  112.8 167.2 %all-gather.8.cloned.1.call-start = ((), (), s32[]{:S(2)}) async-start(), calls=%async_computation.3 | async-start | bytes 8519680 | tf_op jit(solution)/shard_map/all_gather | solution.py:198
Sparse Core Ops, SparseCore 0:
  22.1 85.0 all-gather.3
  112.9 81.5 all-gather.5
  199.2 80.6 all-gather.7

commit v7 on v6

--- a/solution.py
+++ b/solution.py
@@ -24,6 +24,10 @@
         icopies = [pltpu.make_async_copy(r, ini, rsem.at[2]) for r in start_ref]
         for c in icopies:
             c.start()
+        rcopy = pltpu.make_async_copy(r_hbm, rs, rsem.at[0])
+        dcopy = pltpu.make_async_copy(d_hbm, ds, rsem.at[1])
+        rcopy.start()
+        dcopy.start()
         done = per_level * n_early
         ecopies = [
             pltpu.make_async_copy(e, o_ref.at[pl.ds(i * per_level, per_level)], esem.at[i])
@@ -31,8 +35,6 @@
         ]
         for c in ecopies:
             c.start()
-        rcopy = pltpu.make_async_copy(r_hbm, rs, rsem.at[0])
-        dcopy = pltpu.make_async_copy(d_hbm, ds, rsem.at[1])
         slots = []
         for s in range(total):
             b, k = divmod(s, slot_count)
@@ -50,12 +52,6 @@
             def _():
                 pltpu.make_async_copy(f_hbm.at[b, k], fs.at[s], fsem.at[s]).start()
 
-        rcopy.start()
-        dcopy.start()
-        rcopy.wait()
-        dcopy.wait()
-        for c in ecopies:
-            c.wait()
         for c in icopies:
             c.wait()
         for b in range(per_level):
@@ -73,6 +69,11 @@
                     pltpu.make_async_copy(f_hbm.at[0, 0], fs.at[s], fsem.at[s]).wait()
                     acc[...] += jnp.dot(fs[s], xs[s], preferred_element_type=jnp.float32)
 
+            if b == 0:
+                rcopy.wait()
+                dcopy.wait()
+                for c in ecopies:
+                    c.wait()
             residual = (rs[b].astype(jnp.float32) - acc[...]).astype(jnp.bfloat16)
             o_ref[done + b] = jnp.dot(ds[b], residual, preferred_element_type=jnp.float32).astype(o_ref.dtype)
 

time: 292 us -> 291 us (level)
  no operation moved by 1% of the time
where the time goes in v7:
time: 291 us; the launch traced here: 289 us
  waiting for transfers between devices  230 us (79%)
  Pallas kernels  20.3 us (7%)
  between operations  13.2 us (5%)
  blocking collectives  12.6 us (4%)
  local copies, waits for them, and re-layouts  11.5 us (4%)
    all_gather x3, waiting for transfers between devices, shards(): gathered_all.append(lax.all_gather(solved, 'rows', axis=0, tiled=True))  230 us
    pallas_call x3, Pallas kernels, level_solve(): pl.pallas_call(kernel, in_specs=[pl.BlockSpec(memory_space=pltpu.SMEM), a...  13.4 us
    all_to_all x1, blocking collectives, shards(): lax.all_to_all(kernel_rows, 'rhs', split_axis=1, concat_axis=0, tiled=True)  12.6 us
    pallas_call x2, Pallas kernels, partial_sum(): pl.pallas_call(kernel, in_specs=[pl.BlockSpec(memory_space=pltpu.SMEM), a...  6.93 us
  transfers between devices with their start and end apart: 3, of which 3 were waited for; matrix products, arithmetic and copies ran while one was open for 3% of the time, Pallas kernels for 2%

profile of v7, /device:TPU:2, one launch (start us, length us, event | category | flops | bytes accessed | tf_op | source)
XLA Modules:
  0.0 288.7 jit_solution(13877607437823448740)
XLA Ops:
  6.5 0.0 copy-start
  6.5 0.0 copy-start.1
  6.5 0.0 all-gather.4.cloned.1.call-start
  6.6 1.0 copy-done
  7.6 0.1 copy_bitcast_fusion
  7.7 12.6 %all_to_all.16 = bf16[512,4,128]{2,0,1:T(8,128)(2,1)S(1)} all-to-all(bf16[512,4,128]{2,0,1:T(8,128)(2,1)S(1)} %copy_bitcast_fusion), channel_id=1, replica_groups=mesh['rows'=64,'rhs'=4] {'rhs'}, dimensions={1} | all-to-all | bytes 1048576 | tf_op jit(solution)/shard_map/all_to_all | solution.py:154
  20.3 0.8 fusion.16
  21.1 0.0 copy-done.1
  21.1 0.9 convolution_convert_fusion.rest_1_
  22.0 0.0 all-gather.4.cloned.1.call-update
  22.0 0.0 all-gather.6.cloned.1.call-start
  22.1 0.0 copy-done.3
  22.1 0.1 iota_compare_fusion
  22.1 0.0 copy-done.2
  22.2 0.6 reshape.30.table_ref
  22.9 0.9 fusion.15
  23.7 5.7 %fusion.14 = (bf16[2,8,256,256]{3,2,1,0:T(8,128)(2,1)}, bf16[2,8,256,256]{3,2,1,0:T(8,128)(2,1)}, bf16[2,8,256,256]{3,2,1,0:T(8,128)(2,1)}) fusion(bf16[8,8,256,256]{3,2,1,0:T(8,128)(2,1)} %param.6), kind=kLoop, calls=%fused_computation.50 | loop fusion | bytes 12582912 | tf_op jit(solution)/shard_map/slice | solution.py:189
  29.4 77.8 %all-gather.4.cloned.1.call-done.rest_0_ = bf16[128,256,128]{2,1,0:T(8,128)(2,1)} async-done(((bf16[2,256,128]{2,1,0:T(8,128)(2,1)}), bf16[128,256,128]{2,1,0:T(8,128)(2,1)}) %all-gather.4.cloned.1.call-update) | async-done | bytes 8388624 | tf_op jit(solution)/shard_map/all_gather | solution.py:199
  107.2 5.1 %shard_map.55.rest_2_ = bf16[2,256,128]{2,1,0:T(8,128)(2,1)} custom-call(s32[48]{0:T(128)} %reshape.30.table_ref, bf16[2,8,256,256]{3,2,1,0:T(8,128)(2,1)} %get-tuple-element.5.f_hbm, bf16[2,256,128]{2,1,0:T(8,128)(2,1)} %bitcast.38, bf16[2,256,256]{2,1,0:T(8,128)(2,1)} %get-tuple-element.8.d_hbm, bf16[128,256,128]{2,1,0:T(8,128)(2,1)} %all-gather.4.cloned.1.call-done.rest_0_), custom_call_target="tpu_custom_call" | custom-call | tf_op jit(solution)/shard_map/pallas_call | solution.py:81
  112.3 0.0 all-gather.6.cloned.1.call-update
  112.4 0.0 all-gather.8.cloned.1.call-start
  112.4 0.6 reshape.29.table_ref
  113.0 0.7 reshape.31.table_ref
  113.7 3.3 %shard_map.56.rest_1_ = f32[2,256,128]{2,1,0:T(8,128)} custom-call(s32[48]{0:T(128)} %reshape.31.table_ref, bf16[2,8,256,256]{3,2,1,0:T(8,128)(2,1)} %get-tuple-element.7.f_hbm, bf16[128,256,128]{2,1,0:T(8,128)(2,1)} %all-gather.4.cloned.1.call-done.rest_0_), custom_call_target="tpu_custom_call" | custom-call | tf_op jit(solution)/shard_map/pallas_call | solution.py:139
  117.0 75.6 %all-gather.6.cloned.1.call-done.rest_0_.rest_1_ = bf16[128,256,128]{2,1,0:T(8,128)(2,1)} async-done(((bf16[2,256,128]{2,1,0:T(8,128)(2,1)}), bf16[128,256,128]{2,1,0:T(8,128)(2,1)}) %all-gather.6.cloned.1.call-update) | async-done | bytes 8388624 | tf_op jit(solution)/shard_map/all_gather | solution.py:199
  192.6 4.1 %shard_map.57.rest_3_ = bf16[2,256,128]{2,1,0:T(8,128)(2,1)} custom-call(s32[48]{0:T(128)} %reshape.29.table_ref, bf16[2,8,256,256]{3,2,1,0:T(8,128)(2,1)} %get-tuple-element.7.f_hbm, bf16[2,256,128]{2,1,0:T(8,128)(2,1)} %bitcast.37, bf16[2,256,256]{2,1,0:T(8,128)(2,1)} %get-tuple-element.9.d_hbm, ...), custom_call_target="tpu_custom_call" | custom-call | tf_op jit(solution)/shard_map/pallas_call | solution.py:81
  196.7 0.0 all-gather.8.cloned.1.call-update
  196.7 0.6 reshape.32.table_ref
  197.3 0.6 reshape.28.table_ref
  198.0 3.6 %shard_map.58.rest_4_ = f32[2,256,128]{2,1,0:T(8,128)} custom-call(s32[48]{0:T(128)} %reshape.32.table_ref, bf16[2,8,256,256]{3,2,1,0:T(8,128)(2,1)} %get-tuple-element.6.f_hbm, bf16[128,256,128]{2,1,0:T(8,128)(2,1)} %all-gather.4.cloned.1.call-done.rest_0_, bf16[128,256,128]{2,1,0:T(8,128)(2,1)} %all-gather.6.cloned.1.call-done.rest_0_.rest_1_), custom_call_target="tpu_custom_call" | custom-call | tf_op jit(solution)/shard_map/pallas_call | solution.py:139
  201.5 76.4 %all-gather.8.cloned.1.call-done.rest_0_ = bf16[128,256,128]{2,1,0:T(8,128)(2,1)} async-done(((bf16[2,256,128]{2,1,0:T(8,128)(2,1)}), bf16[128,256,128]{2,1,0:T(8,128)(2,1)}) %all-gather.8.cloned.1.call-update) | async-done | bytes 8388624 | tf_op jit(solution)/shard_map/all_gather | solution.py:199
  277.9 4.2 %shard_map.59 = bf16[8,256,128]{2,1,0:T(8,128)(2,1)} custom-call(s32[48]{0:T(128)} %reshape.28.table_ref, bf16[2,8,256,256]{3,2,1,0:T(8,128)(2,1)} %get-tuple-element.6.f_hbm, bf16[2,256,128]{2,1,0:T(8,128)(2,1)} %bitcast.36, bf16[2,256,256]{2,1,0:T(8,128)(2,1)} %get-tuple-element.10.d_hbm, bf16[128,256,128]{2,1,0:T(8,128)(2,1)} %all-gather.8.cloned.1.call-done.rest_0_, ...), custom_call_target="tpu_custom_call" | custom-call | tf_op jit(solution)/shard_map/pallas_call | solution.py:81
  (8 shorter events, 0.1 us)
Async XLA Ops:
  6.5 1.0 copy-start
  6.5 14.5 %copy-start.1 = (bf16[8,256,256]{2,1,0:T(8,128)(2,1)S(1)}, bf16[8,256,256]{2,1,0:T(8,128)(2,1)}, u32[]{:S(2)}) copy-start(bf16[8,256,256]{2,1,0:T(8,128)(2,1)} %param.7) | copy-start | bytes 3145732
  6.5 15.5 %copy-start.3 = (s32[8]{0:T(128)S(1)}, s32[8]{0:T(128)}, u32[]{:S(2)}) copy-start(s32[8]{0:T(128)} %param.9) | copy-start | bytes 100
  6.5 15.6 %copy-start.2 = (s32[8,8]{1,0:T(8,128)S(1)}, s32[8,8]{1,0:T(8,128)}, u32[]{:S(2)}) copy-start(s32[8,8]{1,0:T(8,128)} %param.8) | copy-start | bytes 772
  6.5 100.7 %all-gather.4.cloned.1.call-start = ((), (), s32[]{:S(2)}) async-start(), calls=%async_computation.1 | async-start | bytes 8519680 | tf_op jit(solution)/shard_map/all_gather | solution.py:199
  22.0 170.6 %all-gather.6.cloned.1.call-start = ((), (), s32[]{:S(2)}) async-start(), calls=%async_computation.2 | async-start | bytes 8519680 | tf_op jit(solution)/shard_map/all_gather | solution.py:199
  112.4 165.6 %all-gather.8.cloned.1.call-start = ((), (), s32[]{:S(2)}) async-start(), calls=%async_computation.3 | async-start | bytes 8519680 | tf_op jit(solution)/shard_map/all_gather | solution.py:199
Sparse Core Ops, SparseCore 0:
  22.1 85.0 all-gather.3
  112.5 80.1 all-gather.5
  196.9 81.0 all-gather.7

commit v8 on v7

--- a/solution.py
+++ b/solution.py
@@ -8,8 +8,8 @@
 LEV = 4
 
 
-def level_solve(table, factor, right, dinv, sources, slot_count, earlier=(), init=None):
-    per_level, _, block, _ = factor.shape
+def level_solve(table, factor, right, dinv, sources, slot_count, base, per_level, earlier=(), init=None):
+    block = factor.shape[2]
     width = right.shape[-1]
     n_src = len(sources)
     n_early = len(earlier)
@@ -24,8 +24,8 @@
         icopies = [pltpu.make_async_copy(r, ini, rsem.at[2]) for r in start_ref]
         for c in icopies:
             c.start()
-        rcopy = pltpu.make_async_copy(r_hbm, rs, rsem.at[0])
-        dcopy = pltpu.make_async_copy(d_hbm, ds, rsem.at[1])
+        rcopy = pltpu.make_async_copy(r_hbm.at[pl.ds(base, per_level)], rs, rsem.at[0])
+        dcopy = pltpu.make_async_copy(d_hbm.at[pl.ds(base, per_level)], ds, rsem.at[1])
         rcopy.start()
         dcopy.start()
         done = per_level * n_early
@@ -50,7 +50,7 @@
 
             @pl.when(used)
             def _():
-                pltpu.make_async_copy(f_hbm.at[b, k], fs.at[s], fsem.at[s]).start()
+                pltpu.make_async_copy(f_hbm.at[base + b, k], fs.at[s], fsem.at[s]).start()
 
         for c in icopies:
             c.wait()
@@ -99,8 +99,8 @@
     )(table, factor, right, dinv, *sources, *earlier, *([] if init is None else [init]))
 
 
-def partial_sum(table, factor, sources, slot_count, width):
-    per_level, _, block, _ = factor.shape
+def partial_sum(table, factor, sources, slot_count, width, base, per_level):
+    block = factor.shape[2]
     n_src = len(sources)
     total = per_level * slot_count
 
@@ -122,7 +122,7 @@
 
             @pl.when(used)
             def _():
-                pltpu.make_async_copy(f_hbm.at[b, k], fs.at[s], fsem.at[s]).start()
+                pltpu.make_async_copy(f_hbm.at[base + b, k], fs.at[s], fsem.at[s]).start()
 
         for b in range(per_level):
             o_ref[b] = jnp.zeros((block, width), jnp.float32)
@@ -182,15 +182,19 @@
             init = None
             if newest > 0:
                 old_table = jnp.stack([pos, lv, act]).reshape(-1).astype(jnp.int32)
-                init = partial_sum(old_table, factor_blocks[lower:upper], gathered_all[:newest], slot_count, width)
+                init = partial_sum(
+                    old_table, factor_blocks, gathered_all[:newest], slot_count, width, lower, per_level
+                )
             table = jnp.stack([pos, jnp.where(lv == newest, 0, -1), act]).reshape(-1).astype(jnp.int32)
             solved = level_solve(
                 table,
-                factor_blocks[lower:upper],
-                right_side[lower:upper],
-                diag_inverse[lower:upper],
+                factor_blocks,
+                right_side,
+                diag_inverse,
                 gathered_all[newest:],
                 slot_count,
+                lower,
+                per_level,
                 earlier=tuple(solved_all) if level_now + 1 == LEV else (),
                 init=init,
             )

time: 291 us -> 291 us (level)
  local copies, waits for them, and re-layouts: 11.5 us -> 4.18 us
  waiting for transfers between devices: 230 us -> 233 us
    slice x2 -> x0, local copies, waits for them, and re-layouts: 6.55 us -> none  [the longest x1 5.67 us: shards(): factor_blocks[lower:upper]]
    all_gather x3, waiting for transfers between devices: 230 us -> 233 us  [shards(): gathered_all.append(lax.all_gather(solved, 'rows', axis=0, tiled=True))]
  transfers between devices with their start and end apart: 3 -> 3, of which waited for: 3 -> 3; matrix products, arithmetic and copies ran while one was open for 3% -> 2% of each run, Pallas kernels for 2% -> 2%
where the time goes in v8:
time: 291 us; the launch traced here: 289 us
  waiting for transfers between devices  233 us (80%)
  Pallas kernels  21.9 us (8%)
  between operations  13.2 us (5%)
  blocking collectives  12.6 us (4%)
  local copies, waits for them, and re-layouts  4.18 us (1%)
    all_gather x3, waiting for transfers between devices, shards(): gathered_all.append(lax.all_gather(solved, 'rows', axis=0, tiled=True))  233 us
    pallas_call x3, Pallas kernels, level_solve(): pl.pallas_call(kernel, in_specs=[pl.BlockSpec(memory_space=pltpu.SMEM), a...  15 us
    all_to_all x1, blocking collectives, shards(): lax.all_to_all(kernel_rows, 'rhs', split_axis=1, concat_axis=0, tiled=True)  12.6 us
    pallas_call x2, Pallas kernels, partial_sum(): pl.pallas_call(kernel, in_specs=[pl.BlockSpec(memory_space=pltpu.SMEM), a...  6.92 us
  transfers between devices with their start and end apart: 3, of which 3 were waited for; matrix products, arithmetic and copies ran while one was open for 2% of the time, Pallas kernels for 2%

profile of v8, /device:TPU:2, one launch (start us, length us, event | category | flops | bytes accessed | tf_op | source)
XLA Modules:
  0.0 288.8 jit_solution(10187076299077404606)
XLA Ops:
  6.5 0.0 copy-start
  6.5 0.0 all-gather.4.cloned.1.call-start
  6.5 1.0 copy-done
  7.6 0.1 copy_bitcast_fusion
  7.7 12.6 %all_to_all.16 = bf16[512,4,128]{2,0,1:T(8,128)(2,1)S(1)} all-to-all(bf16[512,4,128]{2,0,1:T(8,128)(2,1)S(1)} %copy_bitcast_fusion), channel_id=1, replica_groups=mesh['rows'=64,'rhs'=4] {'rhs'}, dimensions={1} | all-to-all | bytes 1048576 | tf_op jit(solution)/shard_map/all_to_all | solution.py:154
  20.3 0.0 copy-start.1
  20.3 2.0 convolution_convert_fusion.rest_1_
  22.4 0.0 all-gather.4.cloned.1.call-update
  22.4 0.0 all-gather.6.cloned.1.call-start
  22.4 0.7 iota_compare_fusion
  23.2 0.7 add_select_fusion
  23.9 0.6 reshape.30.table_ref
  24.5 83.1 %all-gather.4.cloned.1.call-done.rest_0_ = bf16[128,256,128]{2,1,0:T(8,128)(2,1)} async-done(((bf16[2,256,128]{2,1,0:T(8,128)(2,1)}), bf16[128,256,128]{2,1,0:T(8,128)(2,1)}) %all-gather.4.cloned.1.call-update) | async-done | bytes 8388624 | tf_op jit(solution)/shard_map/all_gather | solution.py:203
  107.6 0.0 copy-done.1
  107.6 5.6 %shard_map.55.rest_2_ = bf16[2,256,128]{2,1,0:T(8,128)(2,1)} custom-call(s32[48]{0:T(128)} %reshape.30.table_ref, bf16[8,8,256,256]{3,2,1,0:T(8,128)(2,1)} %f_hbm.9, bf16[8,256,128]{2,1,0:T(8,128)(2,1)} %bitcast.35, bf16[8,256,256]{2,1,0:T(8,128)(2,1)} %d_hbm.5, bf16[128,256,128]{2,1,0:T(8,128)(2,1)} %all-gather.4.cloned.1.call-done.rest_0_), custom_call_target="tpu_custom_call" | custom-call | tf_op jit(solution)/shard_map/pallas_call | solution.py:81
  113.2 0.0 all-gather.6.cloned.1.call-update
  113.2 0.0 all-gather.8.cloned.1.call-start
  113.3 0.6 reshape.29.table_ref
  113.9 0.6 reshape.31.table_ref
  114.5 3.7 %shard_map.56.rest_1_ = f32[2,256,128]{2,1,0:T(8,128)} custom-call(s32[48]{0:T(128)} %reshape.31.table_ref, bf16[8,8,256,256]{3,2,1,0:T(8,128)(2,1)} %f_hbm.9, bf16[128,256,128]{2,1,0:T(8,128)(2,1)} %all-gather.4.cloned.1.call-done.rest_0_), custom_call_target="tpu_custom_call" | custom-call | tf_op jit(solution)/shard_map/pallas_call | solution.py:139
  118.2 74.7 %all-gather.6.cloned.1.call-done.rest_0_.rest_1_ = bf16[128,256,128]{2,1,0:T(8,128)(2,1)} async-done(((bf16[2,256,128]{2,1,0:T(8,128)(2,1)}), bf16[128,256,128]{2,1,0:T(8,128)(2,1)}) %all-gather.6.cloned.1.call-update) | async-done | bytes 8388624 | tf_op jit(solution)/shard_map/all_gather | solution.py:203
  192.9 5.1 %shard_map.57.rest_3_ = bf16[2,256,128]{2,1,0:T(8,128)(2,1)} custom-call(s32[48]{0:T(128)} %reshape.29.table_ref, bf16[8,8,256,256]{3,2,1,0:T(8,128)(2,1)} %f_hbm.9, bf16[8,256,128]{2,1,0:T(8,128)(2,1)} %bitcast.36, bf16[8,256,256]{2,1,0:T(8,128)(2,1)} %d_hbm.5, bf16[128,256,128]{2,1,0:T(8,128)(2,1)} %all-gather.6.cloned.1.call-done.rest_0_.rest_1_, ...), custom_call_target="tpu_custom_call" | custom-call | tf_op jit(solution)/shard_map/pallas_call | solution.py:81
  198.0 0.0 all-gather.8.cloned.1.call-update
  198.1 0.6 reshape.32.table_ref
  198.7 0.6 reshape.27.table_ref
  199.3 3.2 %shard_map.58.rest_4_ = f32[2,256,128]{2,1,0:T(8,128)} custom-call(s32[48]{0:T(128)} %reshape.32.table_ref, bf16[8,8,256,256]{3,2,1,0:T(8,128)(2,1)} %f_hbm.9, bf16[128,256,128]{2,1,0:T(8,128)(2,1)} %all-gather.4.cloned.1.call-done.rest_0_, bf16[128,256,128]{2,1,0:T(8,128)(2,1)} %all-gather.6.cloned.1.call-done.rest_0_.rest_1_), custom_call_target="tpu_custom_call" | custom-call | tf_op jit(solution)/shard_map/pallas_call | solution.py:139
  202.5 75.5 %all-gather.8.cloned.1.call-done.rest_0_ = bf16[128,256,128]{2,1,0:T(8,128)(2,1)} async-done(((bf16[2,256,128]{2,1,0:T(8,128)(2,1)}), bf16[128,256,128]{2,1,0:T(8,128)(2,1)}) %all-gather.8.cloned.1.call-update) | async-done | bytes 8388624 | tf_op jit(solution)/shard_map/all_gather | solution.py:203
  278.0 4.2 %shard_map.59 = bf16[8,256,128]{2,1,0:T(8,128)(2,1)} custom-call(s32[48]{0:T(128)} %reshape.27.table_ref, bf16[8,8,256,256]{3,2,1,0:T(8,128)(2,1)} %f_hbm.9, bf16[8,256,128]{2,1,0:T(8,128)(2,1)} %bitcast.37, bf16[8,256,256]{2,1,0:T(8,128)(2,1)} %d_hbm.5, bf16[128,256,128]{2,1,0:T(8,128)(2,1)} %all-gather.8.cloned.1.call-done.rest_0_, ...), custom_call_target="tpu_custom_call" | custom-call | tf_op jit(solution)/shard_map/pallas_call | solution.py:81
  (6 shorter events, 0.0 us)
Async XLA Ops:
  6.5 1.0 copy-start
  6.5 101.1 %all-gather.4.cloned.1.call-start = ((), (), s32[]{:S(2)}) async-start(), calls=%async_computation.1 | async-start | bytes 8519680 | tf_op jit(solution)/shard_map/all_gather | solution.py:203
  20.3 87.3 %copy-start.1 = (bf16[512,4,128]{2,0,1:T(8,128)(2,1)}, bf16[512,4,128]{2,0,1:T(8,128)(2,1)S(1)}, u32[]{:S(2)}) copy-start(bf16[512,4,128]{2,0,1:T(8,128)(2,1)S(1)} %all_to_all.16) | copy-start | bytes 1572868
  22.4 170.5 %all-gather.6.cloned.1.call-start = ((), (), s32[]{:S(2)}) async-start(), calls=%async_computation.2 | async-start | bytes 8519680 | tf_op jit(solution)/shard_map/all_gather | solution.py:203
  113.2 164.7 %all-gather.8.cloned.1.call-start = ((), (), s32[]{:S(2)}) async-start(), calls=%async_computation.3 | async-start | bytes 8519680 | tf_op jit(solution)/shard_map/all_gather | solution.py:203
Sparse Core Ops, SparseCore 0:
  22.5 85.0 all-gather.3
  113.4 79.4 all-gather.5
  198.2 79.7 all-gather.7
